TPU v7x, 32 devices: a whole 2x2x4 slice. The times are simulated.
32 devices in a mesh: segment: 4 (over z), dp: 8 (over y, x, core).
Axes of the slice: x: 2, y: 2, z: 4, core: 2. Of those that a mesh axis runs over, the one named last changes fastest.
Arguments:
- x_in: bfloat16 [2, 512, 8192], P(None, 'dp'), may hold values from -6 to 6
- cotangent: bfloat16 [2, 512, 8192], P(None, 'dp'), may hold values from -6 to 6
- weights: bfloat16 [1024, 128, 128], P('segment'), may hold values from -0.375 to 0.375
- block_index: int32 [1024, 3], P('segment'), may hold values from 0 to 63, as said below
Outputs:
- weight_grad: float32 [1024, 128, 128], P(('segment', 'dp'))
Inputs may be any that keep to these rules, and one draw needn't show every extreme that they name: `block_index`: within each segment's 2 * 128 rows, layer slot j takes rows j * 128 to (j + 1) * 128 - 1. A segment holds 1 to 2 layers, the first ones; the rest have all flags 0; some segment holds 2. A held layer has 32 to 128 kept slots, flags 1 first; some layer keeps 128. The (row, column) pairs of one layer's slots are distinct. Rows and columns of empty slots are arbitrary.
All inputs are finite; a program needn't handle non-finite values.
Results may differ from a plain program's by a relative error of at most 0.013.
Values may be sent and summed in bfloat16 or wider, within the bound.
No kernel may reach another device: no remote copies, remote signals or barrier semaphores. Data moves between devices by JAX's collectives and lax.ppermute only.
A program may use at most 192 MiB of HBM per device.

v0:
```python
import functools

import jax
import jax.numpy as jnp
from jax import lax
from jax.experimental import pallas as pl
from jax.experimental.pallas import tpu as pltpu
from jax.sharding import PartitionSpec as P

BLK = 128
LSLOT = 2
KMAX = 128
CH = 512
NSUB = 16
SPLIT = 2
GROUP = 8
VMEM_LIMIT = 60 * 1024 * 1024

_SMEM = pl.BlockSpec(memory_space=pltpu.SMEM)
_VMEM = pl.BlockSpec(memory_space=pltpu.VMEM)
_ANY = pl.BlockSpec(memory_space=pl.ANY)


def shifted(value, axis, steps):
    count = lax.axis_size(axis)
    leading, last = (max(0, -steps), min(count, count - steps))
    return lax.ppermute(value, axis, [(source, source + steps) for source in range(leading, last)])


def _blk(i):
    return pl.ds(pl.multiple_of(i * BLK, BLK), BLK)


def _chunk(j):
    return pl.ds(pl.multiple_of(j * CH, CH), CH)


def _flag(idx_ref, k):
    return jnp.where(idx_ref[3 * k + 2] > 0, 1.0, 0.0).astype(jnp.float32)


def _w_copies(w_hbm, base, w_vmem, sems):
    copies = []
    for j in range(w_vmem.shape[0] // NSUB):
        copy = pltpu.make_async_copy(
            w_hbm.at[pl.ds(base + j * NSUB, NSUB)], w_vmem.at[pl.ds(j * NSUB, NSUB)], sems.at[j]
        )
        copy.start()
        copies.append(copy)
    return copies


def _slot_chunks(idx_ref, base, copies, product, update):
    for j, copy in enumerate(copies):
        copy.wait()

        @pl.when(idx_ref[3 * (base + j * NSUB) + 2] > 0)
        def _():
            for g in range(j * NSUB, (j + 1) * NSUB, GROUP):
                parts = [product(k) for k in range(g, g + GROUP)]
                for k, part in zip(range(g, g + GROUP), parts):
                    update(k, part)


def _fwd_kernel(base, layer, at_ref, idx_ref, h_ref, w_hbm, sh_in, sy_in, hout_ref, sh_ref, sy_ref, w_vmem, y_vmem, sems, io_sems):
    del sh_in, sy_in
    width = h_ref.shape[1]
    at = at_ref[0]
    copies = _w_copies(w_hbm, base, w_vmem, sems)
    save_h = pltpu.make_async_copy(h_ref, sh_ref.at[layer, at], io_sems.at[0])
    save_h.start()
    y_vmem[...] = jnp.zeros_like(y_vmem)

    def product(k):
        r = idx_ref[3 * (base + k)]
        return jnp.dot(h_ref[:, _blk(r)], w_vmem[k], preferred_element_type=jnp.float32)

    def update(k, p):
        c = idx_ref[3 * (base + k) + 1]
        y_vmem[:, _blk(c)] += p * _flag(idx_ref, base + k)

    _slot_chunks(idx_ref, base, copies, product, update)
    save_y = pltpu.make_async_copy(y_vmem, sy_ref.at[layer, at], io_sems.at[1])
    save_y.start()

    def epi(j, carry):
        y = y_vmem[:, _chunk(j)]
        h = h_ref[:, _chunk(j)].astype(jnp.float32)
        hout_ref[:, _chunk(j)] = (h + y / (1.0 + jnp.exp(-y))).astype(hout_ref.dtype)
        return carry

    lax.fori_loop(0, width // CH, epi, 0)
    save_h.wait()
    save_y.wait()


def layer_forward(h, weights, layer, block_index, at, stash_h, stash_y):
    rows, width = h.shape
    return pl.pallas_call(
        functools.partial(_fwd_kernel, layer * KMAX, layer),
        out_shape=(
            jax.ShapeDtypeStruct((rows, width), jnp.bfloat16),
            jax.ShapeDtypeStruct(stash_h.shape, stash_h.dtype),
            jax.ShapeDtypeStruct(stash_y.shape, stash_y.dtype),
        ),
        in_specs=[_SMEM, _SMEM, _VMEM, _ANY, _ANY, _ANY],
        out_specs=(_VMEM, _ANY, _ANY),
        scratch_shapes=[
            pltpu.VMEM((KMAX, BLK, BLK), weights.dtype),
            pltpu.VMEM((rows, width), jnp.float32),
            pltpu.SemaphoreType.DMA((KMAX // NSUB,)),
            pltpu.SemaphoreType.DMA((2,)),
        ],
        input_output_aliases={4: 1, 5: 2},
        compiler_params=pltpu.CompilerParams(vmem_limit_bytes=VMEM_LIMIT),
    )(at.reshape(1), block_index.reshape(-1), h, weights, stash_h, stash_y)


def _bwd_kernel(base, layer, at_ref, idx_ref, g_ref, sy_hbm, w_hbm, ss_in, gout_ref, ss_ref, y_vmem, s_vmem, sp_ref, w_vmem, sems, io_sems):
    del ss_in
    width = g_ref.shape[1]
    at = at_ref[0]
    load_y = pltpu.make_async_copy(sy_hbm.at[layer, at], y_vmem, io_sems.at[0])
    load_y.start()
    copies = _w_copies(w_hbm, base, w_vmem, sems)
    load_y.wait()

    def pre(j, carry):
        y = y_vmem[:, _chunk(j)]
        sig = 1.0 / (1.0 + jnp.exp(-y))
        g = g_ref[:, _chunk(j)].astype(jnp.float32)
        s_vmem[:, _chunk(j)] = (g * sig * (1.0 + y * (1.0 - sig))).astype(s_vmem.dtype)
        sp_ref[:, _chunk(j)] = jnp.zeros((g_ref.shape[0], CH), jnp.float32)
        return carry

    lax.fori_loop(0, width // CH, pre, 0)
    save_s = pltpu.make_async_copy(s_vmem, ss_ref.at[layer, at], io_sems.at[1])
    save_s.start()

    def product(k):
        c = idx_ref[3 * (base + k) + 1]
        return lax.dot_general(
            s_vmem[:, _blk(c)],
            w_vmem[k],
            (((1,), (1,)), ((), ())),
            preferred_element_type=jnp.float32,
        )

    def update(k, back):
        r = idx_ref[3 * (base + k)]
        sp_ref[:, _blk(r)] += back * _flag(idx_ref, base + k)

    _slot_chunks(idx_ref, base, copies, product, update)

    def epi(j, carry):
        g = g_ref[:, _chunk(j)].astype(jnp.float32)
        gout_ref[:, _chunk(j)] = (g + sp_ref[:, _chunk(j)]).astype(gout_ref.dtype)
        return carry

    lax.fori_loop(0, width // CH, epi, 0)
    save_s.wait()


def layer_backward(g, stash_y, weights, layer, block_index, at, stash_s):
    rows, width = g.shape
    return pl.pallas_call(
        functools.partial(_bwd_kernel, layer * KMAX, layer),
        out_shape=(
            jax.ShapeDtypeStruct((rows, width), jnp.bfloat16),
            jax.ShapeDtypeStruct(stash_s.shape, stash_s.dtype),
        ),
        in_specs=[_SMEM, _SMEM, _VMEM, _ANY, _ANY, _ANY],
        out_specs=(_VMEM, _ANY),
        scratch_shapes=[
            pltpu.VMEM((rows, width), jnp.float32),
            pltpu.VMEM((rows, width), jnp.bfloat16),
            pltpu.VMEM((rows, width), jnp.float32),
            pltpu.VMEM((KMAX, BLK, BLK), weights.dtype),
            pltpu.SemaphoreType.DMA((KMAX // NSUB,)),
            pltpu.SemaphoreType.DMA((2,)),
        ],
        input_output_aliases={5: 1},
        compiler_params=pltpu.CompilerParams(vmem_limit_bytes=VMEM_LIMIT),
    )(at.reshape(1), block_index.reshape(-1), g, stash_y, weights, stash_s)


def _dw_kernel(mbs, idx_ref, h_ref, s_ref, dw_ref):
    rows = h_ref.shape[1] * h_ref.shape[2]
    for j in range(dw_ref.shape[0] // NSUB):
        layer = j * NSUB // KMAX

        @pl.when(idx_ref[3 * j * NSUB + 2] > 0)
        def _():
            for k in range(j * NSUB, (j + 1) * NSUB):
                r = idx_ref[3 * k]
                c = idx_ref[3 * k + 1]
                hb = h_ref[layer, :, :, _blk(r)]
                sb = s_ref[layer, :, :, _blk(c)]
                dw_ref[k] = lax.dot_general(
                    hb.reshape(rows, BLK),
                    sb.reshape(rows, BLK),
                    (((0,), (0,)), ((), ())),
                    preferred_element_type=jnp.float32,
                ) * _flag(idx_ref, k)

        @pl.when(idx_ref[3 * j * NSUB + 2] <= 0)
        def _():
            dw_ref[pl.ds(j * NSUB, NSUB)] = jnp.zeros((NSUB, BLK, BLK), jnp.float32)


def segment_dw(stash_h, stash_s, block_index, mbs):
    return pl.pallas_call(
        functools.partial(_dw_kernel, mbs),
        out_shape=jax.ShapeDtypeStruct((block_index.shape[0], BLK, BLK), jnp.float32),
        in_specs=[_SMEM, _VMEM, _VMEM],
        out_specs=_VMEM,
        compiler_params=pltpu.CompilerParams(vmem_limit_bytes=VMEM_LIMIT),
    )(block_index.reshape(-1), stash_h, stash_s)


def _exchange(send, pairs):
    return lax.ppermute(send.astype(jnp.bfloat16), "dp", pairs).astype(jnp.float32)


def dp_reduce_scatter(acc):
    n = lax.axis_size("dp")
    if n != 8:
        return lax.psum_scatter(
            acc.astype(jnp.bfloat16), "dp", scatter_dimension=0, tiled=True
        ).astype(jnp.float32)
    d = lax.axis_index("dp")
    d0, d1, d2 = d % 2, (d // 2) % 2, d // 4
    pick = lambda a, i, axis: lax.dynamic_index_in_dim(a, i, axis, keepdims=False)
    x = acc.reshape((2, 2, 2, acc.shape[0] // 8) + acc.shape[1:])
    x = pick(x, d0, 2) + _exchange(pick(x, 1 - d0, 2), [(i, i ^ 1) for i in range(8)])
    core0 = d0 == 0
    keep = jnp.where(core0, pick(x, d1, 1), pick(x, d2, 0))
    send = jnp.where(core0, pick(x, 1 - d1, 1), pick(x, 1 - d2, 0))
    x = keep + _exchange(send, [(i, i ^ (2 if i % 2 == 0 else 4)) for i in range(8)])
    rem = jnp.where(core0, d2, d1)
    send = pick(x, 1 - rem, 0)
    return pick(x, rem, 0) + _exchange(send, [(i, i ^ (4 if i % 2 == 0 else 2)) for i in range(8)])


def on_device(x_in, cotangent, weights, block_index):
    segments = lax.axis_size("segment")
    me_segment = lax.axis_index("segment")
    mbs, rows_dev, width = x_in.shape
    mbs, rows_dev = mbs * SPLIT, rows_dev // SPLIT
    x_in = x_in.reshape(mbs, rows_dev, width)
    cotangent = cotangent.reshape(mbs, rows_dev, width)
    idx = block_index.reshape(LSLOT, KMAX, 3)
    ticks = mbs + segments - 1

    def forward_tick(tick, carry):
        received, saved_h, saved_y = carry
        micro = tick - me_segment
        live = (micro >= 0) & (micro < mbs)
        place_at = jnp.clip(micro, 0, mbs - 1)
        first = lax.dynamic_index_in_dim(x_in, place_at, 0, keepdims=False)
        start = jnp.where(me_segment == 0, first, received)

        def run(operands):
            h, sh, sy = operands
            for layer in range(LSLOT):
                h, sh, sy = layer_forward(h, weights, layer, block_index, place_at, sh, sy)
            return (h, sh, sy)

        h_out, saved_h, saved_y = lax.cond(live, run, lambda ops: ops, (start, saved_h, saved_y))
        received = shifted(h_out, "segment", 1)
        return (received, saved_h, saved_y)

    stash_h = jnp.zeros((LSLOT, mbs, rows_dev, width), jnp.bfloat16)
    stash_y = jnp.zeros((LSLOT, mbs, rows_dev, width), jnp.float32)
    blank = jnp.zeros((rows_dev, width), jnp.bfloat16)
    unused_recv, stash_h, stash_y = lax.fori_loop(
        0, ticks, forward_tick, (blank, stash_h, stash_y)
    )
    stash_s = jnp.zeros((LSLOT, mbs, rows_dev, width), jnp.bfloat16)

    def backward_tick(tick, carry):
        received, saved_s = carry
        micro = tick - (segments - 1 - me_segment)
        live = (micro >= 0) & (micro < mbs)
        place_at = jnp.clip(micro, 0, mbs - 1)
        top = lax.dynamic_index_in_dim(cotangent, place_at, 0, keepdims=False)
        grad_in = jnp.where(me_segment == segments - 1, top, received)

        def run(operands):
            grad, ss = operands
            for layer in reversed(range(LSLOT)):
                grad, ss = layer_backward(grad, stash_y, weights, layer, block_index, place_at, ss)
            return (grad, ss)

        grad_out, saved_s = lax.cond(live, run, lambda ops: ops, (grad_in, saved_s))
        received = shifted(grad_out, "segment", -1)
        return (received, saved_s)

    unused_grad, stash_s = lax.fori_loop(0, ticks, backward_tick, (blank, stash_s))
    acc = segment_dw(stash_h, stash_s, block_index, mbs)
    return dp_reduce_scatter(acc)


def solution(mesh):
    return jax.shard_map(
        on_device,
        mesh=mesh,
        in_specs=(
            P(None, "dp", None),
            P(None, "dp", None),
            P("segment", None, None),
            P("segment", None),
        ),
        out_specs=P(("segment", "dp"), None, None),
        check_vma=False,
    )
```

profile of v0, /device:TPU:0, one launch (start us, length us, event | category | flops | bytes accessed | tf_op | source)
XLA Modules:
  0.0 459.0 jit_solution(12799702410089632994)
XLA Ops:
  8.3 164.8 %while.35 = (s32[]{:T(128)}, bf16[32,8192]{1,0:T(8,128)(2,1)S(1)}, bf16[2,4,32,8192]{3,2,1,0:T(8,128)(2,1)}, f32[2,4,32,8192]{3,2,1,0:T(8,128)}, s32[]{:T(128)},...) while((s32[]{:T(128)}, bf16[32,8192]{1,0:T(8,128)(2,1)S(1)}, ...), condition=%wide.region_3.4_spmd, body=%wide.region_0.3_spmd.sunk | while | flops 262153 | bytes 3676472 | solution.py:276
  9.4 10.2 %conditional.4 = ((bf16[32,8192]{1,0:T(8,128)(2,1)S(1)}, bf16[2,4,32,8192]{3,2,1,0:T(8,128)(2,1)}, f32[2,4,32,8192]{3,2,1,0:T(8,128)})) conditional(s32[]{:T(128)} %convert_element_type.61, (bf16[32,8192]{1,0:T(8,128)(2,1)S(1)}, bf16[2,4,32,8192]{3,2,1,0:T(8,128)(2,1)}, f32[2,4,32,8192]{3,2,1,0:T(8,128)}) %tuple.81, (s32[]{:T(128)}, ...), branch_computations={%region_1.1_spmd, %region_2.2_spmd} | conditional | bytes 6152 | solution.py:269
  10.3 4.9 %branch_1_fun.4 = (bf16[32,8192]{1,0:T(8,128)(2,1)}, bf16[2,4,32,8192]{3,2,1,0:T(8,128)(2,1)}, f32[2,4,32,8192]{3,2,1,0:T(8,128)}) custom-call(s32[1]{0:T(128)} %bitcast.at_ref, s32[768]{0:T(1024)} %reshape.19.idx_ref, bf16[32,8192]{1,0:T(8,128)(2,1)S(1)} %get-tuple-element.401.h_ref, ...), custom_call_target="tpu_custom_call", output_to_operand_aliasing={{1}: (4, {}), {2}: (5, {})} | custom-call | tf_op jit(solution)/shard_map/while/body/eval_jaxpr/cond/branch_1_fun/pallas_call | solution.py:99
  21.0 12.0 %collective-permute-done = bf16[32,8192]{1,0:T(8,128)(2,1)S(1)} collective-permute-done((bf16[32,8192]{1,0:T(8,128)(2,1)S(1)}, bf16[32,8192]{1,0:T(8,128)(2,1)S(1)}, u32[]{:S(2)}, u32[]{:S(2)}) %collective-permute-start) | collective-permute-done | bytes 524320 | tf_op jit(solution)/shard_map/while/body/eval_jaxpr/ppermute | solution.py:27
  34.1 10.2 %conditional.4 = ((bf16[32,8192]{1,0:T(8,128)(2,1)S(1)}, bf16[2,4,32,8192]{3,2,1,0:T(8,128)(2,1)}, f32[2,4,32,8192]{3,2,1,0:T(8,128)})) conditional(s32[]{:T(128)} %convert_element_type.61, (bf16[32,8192]{1,0:T(8,128)(2,1)S(1)}, bf16[2,4,32,8192]{3,2,1,0:T(8,128)(2,1)}, f32[2,4,32,8192]{3,2,1,0:T(8,128)}) %tuple.81, (s32[]{:T(128)}, ...), branch_computations={%region_1.1_spmd, %region_2.2_spmd} | conditional | bytes 6152 | solution.py:269
  34.9 4.9 %branch_1_fun.4 = (bf16[32,8192]{1,0:T(8,128)(2,1)}, bf16[2,4,32,8192]{3,2,1,0:T(8,128)(2,1)}, f32[2,4,32,8192]{3,2,1,0:T(8,128)}) custom-call(s32[1]{0:T(128)} %bitcast.at_ref, s32[768]{0:T(1024)} %reshape.19.idx_ref, bf16[32,8192]{1,0:T(8,128)(2,1)S(1)} %get-tuple-element.401.h_ref, ...), custom_call_target="tpu_custom_call", output_to_operand_aliasing={{1}: (4, {}), {2}: (5, {})} | custom-call | tf_op jit(solution)/shard_map/while/body/eval_jaxpr/cond/branch_1_fun/pallas_call | solution.py:99
  44.3 5.4 %collective-permute-start = (bf16[32,8192]{1,0:T(8,128)(2,1)S(1)}, bf16[32,8192]{1,0:T(8,128)(2,1)S(1)}, u32[]{:S(2)}, u32[]{:S(2)}) collective-permute-start(bf16[32,8192]{1,0:T(8,128)(2,1)S(1)} %get-tuple-element.625), channel_id=1, source_target_pairs={{0,8},{8,16},{16,24},{1,9},{9,17},{17,25},{2,10},{10,18},{18,26},{... | collective-permute-start | bytes 1572872 | tf_op jit(solution)/shard_map/while/body/eval_jaxpr/ppermute | solution.py:27
  49.7 11.2 %collective-permute-done = bf16[32,8192]{1,0:T(8,128)(2,1)S(1)} collective-permute-done((bf16[32,8192]{1,0:T(8,128)(2,1)S(1)}, bf16[32,8192]{1,0:T(8,128)(2,1)S(1)}, u32[]{:S(2)}, u32[]{:S(2)}) %collective-permute-start) | collective-permute-done | bytes 524320 | tf_op jit(solution)/shard_map/while/body/eval_jaxpr/ppermute | solution.py:27
  62.0 10.2 %conditional.4 = ((bf16[32,8192]{1,0:T(8,128)(2,1)S(1)}, bf16[2,4,32,8192]{3,2,1,0:T(8,128)(2,1)}, f32[2,4,32,8192]{3,2,1,0:T(8,128)})) conditional(s32[]{:T(128)} %convert_element_type.61, (bf16[32,8192]{1,0:T(8,128)(2,1)S(1)}, bf16[2,4,32,8192]{3,2,1,0:T(8,128)(2,1)}, f32[2,4,32,8192]{3,2,1,0:T(8,128)}) %tuple.81, (s32[]{:T(128)}, ...), branch_computations={%region_1.1_spmd, %region_2.2_spmd} | conditional | bytes 6152 | solution.py:269
  62.8 4.9 %branch_1_fun.4 = (bf16[32,8192]{1,0:T(8,128)(2,1)}, bf16[2,4,32,8192]{3,2,1,0:T(8,128)(2,1)}, f32[2,4,32,8192]{3,2,1,0:T(8,128)}) custom-call(s32[1]{0:T(128)} %bitcast.at_ref, s32[768]{0:T(1024)} %reshape.19.idx_ref, bf16[32,8192]{1,0:T(8,128)(2,1)S(1)} %get-tuple-element.401.h_ref, ...), custom_call_target="tpu_custom_call", output_to_operand_aliasing={{1}: (4, {}), {2}: (5, {})} | custom-call | tf_op jit(solution)/shard_map/while/body/eval_jaxpr/cond/branch_1_fun/pallas_call | solution.py:99
  72.1 5.4 %collective-permute-start = (bf16[32,8192]{1,0:T(8,128)(2,1)S(1)}, bf16[32,8192]{1,0:T(8,128)(2,1)S(1)}, u32[]{:S(2)}, u32[]{:S(2)}) collective-permute-start(bf16[32,8192]{1,0:T(8,128)(2,1)S(1)} %get-tuple-element.625), channel_id=1, source_target_pairs={{0,8},{8,16},{16,24},{1,9},{9,17},{17,25},{2,10},{10,18},{18,26},{... | collective-permute-start | bytes 1572872 | tf_op jit(solution)/shard_map/while/body/eval_jaxpr/ppermute | solution.py:27
  77.6 10.3 %collective-permute-done = bf16[32,8192]{1,0:T(8,128)(2,1)S(1)} collective-permute-done((bf16[32,8192]{1,0:T(8,128)(2,1)S(1)}, bf16[32,8192]{1,0:T(8,128)(2,1)S(1)}, u32[]{:S(2)}, u32[]{:S(2)}) %collective-permute-start) | collective-permute-done | bytes 524320 | tf_op jit(solution)/shard_map/while/body/eval_jaxpr/ppermute | solution.py:27
  89.0 10.3 %conditional.4 = ((bf16[32,8192]{1,0:T(8,128)(2,1)S(1)}, bf16[2,4,32,8192]{3,2,1,0:T(8,128)(2,1)}, f32[2,4,32,8192]{3,2,1,0:T(8,128)})) conditional(s32[]{:T(128)} %convert_element_type.61, (bf16[32,8192]{1,0:T(8,128)(2,1)S(1)}, bf16[2,4,32,8192]{3,2,1,0:T(8,128)(2,1)}, f32[2,4,32,8192]{3,2,1,0:T(8,128)}) %tuple.81, (s32[]{:T(128)}, ...), branch_computations={%region_1.1_spmd, %region_2.2_spmd} | conditional | bytes 6152 | solution.py:269
  89.8 4.9 %branch_1_fun.4 = (bf16[32,8192]{1,0:T(8,128)(2,1)}, bf16[2,4,32,8192]{3,2,1,0:T(8,128)(2,1)}, f32[2,4,32,8192]{3,2,1,0:T(8,128)}) custom-call(s32[1]{0:T(128)} %bitcast.at_ref, s32[768]{0:T(1024)} %reshape.19.idx_ref, bf16[32,8192]{1,0:T(8,128)(2,1)S(1)} %get-tuple-element.401.h_ref, ...), custom_call_target="tpu_custom_call", output_to_operand_aliasing={{1}: (4, {}), {2}: (5, {})} | custom-call | tf_op jit(solution)/shard_map/while/body/eval_jaxpr/cond/branch_1_fun/pallas_call | solution.py:99
  99.3 5.3 %collective-permute-start = (bf16[32,8192]{1,0:T(8,128)(2,1)S(1)}, bf16[32,8192]{1,0:T(8,128)(2,1)S(1)}, u32[]{:S(2)}, u32[]{:S(2)}) collective-permute-start(bf16[32,8192]{1,0:T(8,128)(2,1)S(1)} %get-tuple-element.625), channel_id=1, source_target_pairs={{0,8},{8,16},{16,24},{1,9},{9,17},{17,25},{2,10},{10,18},{18,26},{... | collective-permute-start | bytes 1572872 | tf_op jit(solution)/shard_map/while/body/eval_jaxpr/ppermute | solution.py:27
  104.6 9.4 %collective-permute-done = bf16[32,8192]{1,0:T(8,128)(2,1)S(1)} collective-permute-done((bf16[32,8192]{1,0:T(8,128)(2,1)S(1)}, bf16[32,8192]{1,0:T(8,128)(2,1)S(1)}, u32[]{:S(2)}, u32[]{:S(2)}) %collective-permute-start) | collective-permute-done | bytes 524320 | tf_op jit(solution)/shard_map/while/body/eval_jaxpr/ppermute | solution.py:27
  115.1 15.7 %collective-permute-start = (bf16[32,8192]{1,0:T(8,128)(2,1)S(1)}, bf16[32,8192]{1,0:T(8,128)(2,1)S(1)}, u32[]{:S(2)}, u32[]{:S(2)}) collective-permute-start(bf16[32,8192]{1,0:T(8,128)(2,1)S(1)} %get-tuple-element.625), channel_id=1, source_target_pairs={{0,8},{8,16},{16,24},{1,9},{9,17},{17,25},{2,10},{10,18},{18,26},{... | collective-permute-start | bytes 1572872 | tf_op jit(solution)/shard_map/while/body/eval_jaxpr/ppermute | solution.py:27
  130.8 8.5 %collective-permute-done = bf16[32,8192]{1,0:T(8,128)(2,1)S(1)} collective-permute-done((bf16[32,8192]{1,0:T(8,128)(2,1)S(1)}, bf16[32,8192]{1,0:T(8,128)(2,1)S(1)}, u32[]{:S(2)}, u32[]{:S(2)}) %collective-permute-start) | collective-permute-done | bytes 524320 | tf_op jit(solution)/shard_map/while/body/eval_jaxpr/ppermute | solution.py:27
  144.8 7.5 %collective-permute-done = bf16[32,8192]{1,0:T(8,128)(2,1)S(1)} collective-permute-done((bf16[32,8192]{1,0:T(8,128)(2,1)S(1)}, bf16[32,8192]{1,0:T(8,128)(2,1)S(1)}, u32[]{:S(2)}, u32[]{:S(2)}) %collective-permute-start) | collective-permute-done | bytes 524320 | tf_op jit(solution)/shard_map/while/body/eval_jaxpr/ppermute | solution.py:27
  153.4 12.8 %collective-permute-start = (bf16[32,8192]{1,0:T(8,128)(2,1)S(1)}, bf16[32,8192]{1,0:T(8,128)(2,1)S(1)}, u32[]{:S(2)}, u32[]{:S(2)}) collective-permute-start(bf16[32,8192]{1,0:T(8,128)(2,1)S(1)} %get-tuple-element.625), channel_id=1, source_target_pairs={{0,8},{8,16},{16,24},{1,9},{9,17},{17,25},{2,10},{10,18},{18,26},{... | collective-permute-start | bytes 1572872 | tf_op jit(solution)/shard_map/while/body/eval_jaxpr/ppermute | solution.py:27
  166.2 6.9 %collective-permute-done = bf16[32,8192]{1,0:T(8,128)(2,1)S(1)} collective-permute-done((bf16[32,8192]{1,0:T(8,128)(2,1)S(1)}, bf16[32,8192]{1,0:T(8,128)(2,1)S(1)}, u32[]{:S(2)}, u32[]{:S(2)}) %collective-permute-start) | collective-permute-done | bytes 524320 | tf_op jit(solution)/shard_map/while/body/eval_jaxpr/ppermute | solution.py:27
  175.6 194.4 %while.36 = (s32[]{:T(128)}, bf16[32,8192]{1,0:T(8,128)(2,1)S(1)}, bf16[2,4,32,8192]{3,2,1,0:T(8,128)(2,1)}, s32[]{:T(128)}, pred[]{:T(512)}, /*index=5*/bf16[4,...) while((s32[]{:T(128)}, bf16[32,8192]{1,0:T(8,128)(2,1)S(1)}, ...), condition=%wide.region_7.8_spmd, body=%wide.region_4.7_spmd.sunk | while | flops 262153 | bytes 3676464 | solution.py:299
  178.1 10.2 %collective-permute-done.1 = bf16[32,8192]{1,0:T(8,128)(2,1)S(1)} collective-permute-done((bf16[32,8192]{1,0:T(8,128)(2,1)S(1)}, bf16[32,8192]{1,0:T(8,128)(2,1)S(1)}, u32[]{:S(2)}, u32[]{:S(2)}) %collective-permute-start.1) | collective-permute-done | bytes 524320 | tf_op jit(solution)/shard_map/while/body/eval_jaxpr/ppermute | solution.py:27
  190.7 21.3 %collective-permute-done.1 = bf16[32,8192]{1,0:T(8,128)(2,1)S(1)} collective-permute-done((bf16[32,8192]{1,0:T(8,128)(2,1)S(1)}, bf16[32,8192]{1,0:T(8,128)(2,1)S(1)}, u32[]{:S(2)}, u32[]{:S(2)}) %collective-permute-start.1) | collective-permute-done | bytes 524320 | tf_op jit(solution)/shard_map/while/body/eval_jaxpr/ppermute | solution.py:27
  214.5 49.8 %collective-permute-done.1 = bf16[32,8192]{1,0:T(8,128)(2,1)S(1)} collective-permute-done((bf16[32,8192]{1,0:T(8,128)(2,1)S(1)}, bf16[32,8192]{1,0:T(8,128)(2,1)S(1)}, u32[]{:S(2)}, u32[]{:S(2)}) %collective-permute-start.1) | collective-permute-done | bytes 524320 | tf_op jit(solution)/shard_map/while/body/eval_jaxpr/ppermute | solution.py:27
  265.4 12.8 %conditional.5 = ((bf16[32,8192]{1,0:T(8,128)(2,1)S(1)}, bf16[2,4,32,8192]{3,2,1,0:T(8,128)(2,1)})) conditional(s32[]{:T(128)} %convert_element_type.62, (bf16[32,8192]{1,0:T(8,128)(2,1)S(1)}, bf16[2,4,32,8192]{3,2,1,0:T(8,128)(2,1)}) %tuple.84, (s32[]{:T(128)}, s32[256,3]{1,0:T(8,128)S(1)}, bf16[32,8192]{1,0:T(8,128)(2,1)S(1)}, ...), branch_computations={%region_5.5_spmd, %region_6.6_spmd} | conditional | bytes 6152 | solution.py:295
  266.2 6.4 %branch_1_fun.6 = (bf16[32,8192]{1,0:T(8,128)(2,1)}, bf16[2,4,32,8192]{3,2,1,0:T(8,128)(2,1)}) custom-call(s32[1]{0:T(128)} %bitcast.2.at_ref, s32[768]{0:T(1024)} %reshape.25.idx_ref, bf16[32,8192]{1,0:T(8,128)(2,1)S(1)} %get-tuple-element.423.g_ref, f32[2,4,32,8192]{3,2,1,0:T(8,128)} %get-tuple-element.424.sy_hbm, ...), custom_call_target="tpu_custom_call", output_to_operand_aliasing={{1}: (5, {})} | custom-call | tf_op jit(solution)/shard_map/while/body/eval_jaxpr/cond/branch_1_fun/pallas_call | solution.py:166
  272.6 5.6 %branch_1_fun.7 = (bf16[32,8192]{1,0:T(8,128)(2,1)S(1)}, bf16[2,4,32,8192]{3,2,1,0:T(8,128)(2,1)}) custom-call(s32[1]{0:T(128)} %bitcast.2.at_ref, s32[768]{0:T(1024)} %reshape.25.idx_ref, bf16[32,8192]{1,0:T(8,128)(2,1)} %get-tuple-element.427.g_ref, f32[2,4,32,8192]{3,2,1,0:T(8,128)} %get-tuple-element.424.sy_hbm, ...), custom_call_target="tpu_custom_call", output_to_operand_aliasing={{1}: (5, {})} | custom-call | tf_op jit(solution)/shard_map/while/body/eval_jaxpr/cond/branch_1_fun/pallas_call | solution.py:166
  279.5 11.7 %collective-permute-done.1 = bf16[32,8192]{1,0:T(8,128)(2,1)S(1)} collective-permute-done((bf16[32,8192]{1,0:T(8,128)(2,1)S(1)}, bf16[32,8192]{1,0:T(8,128)(2,1)S(1)}, u32[]{:S(2)}, u32[]{:S(2)}) %collective-permute-start.1) | collective-permute-done | bytes 524320 | tf_op jit(solution)/shard_map/while/body/eval_jaxpr/ppermute | solution.py:27
  292.3 12.8 %conditional.5 = ((bf16[32,8192]{1,0:T(8,128)(2,1)S(1)}, bf16[2,4,32,8192]{3,2,1,0:T(8,128)(2,1)})) conditional(s32[]{:T(128)} %convert_element_type.62, (bf16[32,8192]{1,0:T(8,128)(2,1)S(1)}, bf16[2,4,32,8192]{3,2,1,0:T(8,128)(2,1)}) %tuple.84, (s32[]{:T(128)}, s32[256,3]{1,0:T(8,128)S(1)}, bf16[32,8192]{1,0:T(8,128)(2,1)S(1)}, ...), branch_computations={%region_5.5_spmd, %region_6.6_spmd} | conditional | bytes 6152 | solution.py:295
  293.2 6.4 %branch_1_fun.6 = (bf16[32,8192]{1,0:T(8,128)(2,1)}, bf16[2,4,32,8192]{3,2,1,0:T(8,128)(2,1)}) custom-call(s32[1]{0:T(128)} %bitcast.2.at_ref, s32[768]{0:T(1024)} %reshape.25.idx_ref, bf16[32,8192]{1,0:T(8,128)(2,1)S(1)} %get-tuple-element.423.g_ref, f32[2,4,32,8192]{3,2,1,0:T(8,128)} %get-tuple-element.424.sy_hbm, ...), custom_call_target="tpu_custom_call", output_to_operand_aliasing={{1}: (5, {})} | custom-call | tf_op jit(solution)/shard_map/while/body/eval_jaxpr/cond/branch_1_fun/pallas_call | solution.py:166
  299.6 5.6 %branch_1_fun.7 = (bf16[32,8192]{1,0:T(8,128)(2,1)S(1)}, bf16[2,4,32,8192]{3,2,1,0:T(8,128)(2,1)}) custom-call(s32[1]{0:T(128)} %bitcast.2.at_ref, s32[768]{0:T(1024)} %reshape.25.idx_ref, bf16[32,8192]{1,0:T(8,128)(2,1)} %get-tuple-element.427.g_ref, f32[2,4,32,8192]{3,2,1,0:T(8,128)} %get-tuple-element.424.sy_hbm, ...), custom_call_target="tpu_custom_call", output_to_operand_aliasing={{1}: (5, {})} | custom-call | tf_op jit(solution)/shard_map/while/body/eval_jaxpr/cond/branch_1_fun/pallas_call | solution.py:166
  306.4 11.7 %collective-permute-done.1 = bf16[32,8192]{1,0:T(8,128)(2,1)S(1)} collective-permute-done((bf16[32,8192]{1,0:T(8,128)(2,1)S(1)}, bf16[32,8192]{1,0:T(8,128)(2,1)S(1)}, u32[]{:S(2)}, u32[]{:S(2)}) %collective-permute-start.1) | collective-permute-done | bytes 524320 | tf_op jit(solution)/shard_map/while/body/eval_jaxpr/ppermute | solution.py:27
  319.3 12.8 %conditional.5 = ((bf16[32,8192]{1,0:T(8,128)(2,1)S(1)}, bf16[2,4,32,8192]{3,2,1,0:T(8,128)(2,1)})) conditional(s32[]{:T(128)} %convert_element_type.62, (bf16[32,8192]{1,0:T(8,128)(2,1)S(1)}, bf16[2,4,32,8192]{3,2,1,0:T(8,128)(2,1)}) %tuple.84, (s32[]{:T(128)}, s32[256,3]{1,0:T(8,128)S(1)}, bf16[32,8192]{1,0:T(8,128)(2,1)S(1)}, ...), branch_computations={%region_5.5_spmd, %region_6.6_spmd} | conditional | bytes 6152 | solution.py:295
  320.1 6.4 %branch_1_fun.6 = (bf16[32,8192]{1,0:T(8,128)(2,1)}, bf16[2,4,32,8192]{3,2,1,0:T(8,128)(2,1)}) custom-call(s32[1]{0:T(128)} %bitcast.2.at_ref, s32[768]{0:T(1024)} %reshape.25.idx_ref, bf16[32,8192]{1,0:T(8,128)(2,1)S(1)} %get-tuple-element.423.g_ref, f32[2,4,32,8192]{3,2,1,0:T(8,128)} %get-tuple-element.424.sy_hbm, ...), custom_call_target="tpu_custom_call", output_to_operand_aliasing={{1}: (5, {})} | custom-call | tf_op jit(solution)/shard_map/while/body/eval_jaxpr/cond/branch_1_fun/pallas_call | solution.py:166
  326.5 5.6 %branch_1_fun.7 = (bf16[32,8192]{1,0:T(8,128)(2,1)S(1)}, bf16[2,4,32,8192]{3,2,1,0:T(8,128)(2,1)}) custom-call(s32[1]{0:T(128)} %bitcast.2.at_ref, s32[768]{0:T(1024)} %reshape.25.idx_ref, bf16[32,8192]{1,0:T(8,128)(2,1)} %get-tuple-element.427.g_ref, f32[2,4,32,8192]{3,2,1,0:T(8,128)} %get-tuple-element.424.sy_hbm, ...), custom_call_target="tpu_custom_call", output_to_operand_aliasing={{1}: (5, {})} | custom-call | tf_op jit(solution)/shard_map/while/body/eval_jaxpr/cond/branch_1_fun/pallas_call | solution.py:166
  333.4 11.7 %collective-permute-done.1 = bf16[32,8192]{1,0:T(8,128)(2,1)S(1)} collective-permute-done((bf16[32,8192]{1,0:T(8,128)(2,1)S(1)}, bf16[32,8192]{1,0:T(8,128)(2,1)S(1)}, u32[]{:S(2)}, u32[]{:S(2)}) %collective-permute-start.1) | collective-permute-done | bytes 524320 | tf_op jit(solution)/shard_map/while/body/eval_jaxpr/ppermute | solution.py:27
  346.2 12.8 %conditional.5 = ((bf16[32,8192]{1,0:T(8,128)(2,1)S(1)}, bf16[2,4,32,8192]{3,2,1,0:T(8,128)(2,1)})) conditional(s32[]{:T(128)} %convert_element_type.62, (bf16[32,8192]{1,0:T(8,128)(2,1)S(1)}, bf16[2,4,32,8192]{3,2,1,0:T(8,128)(2,1)}) %tuple.84, (s32[]{:T(128)}, s32[256,3]{1,0:T(8,128)S(1)}, bf16[32,8192]{1,0:T(8,128)(2,1)S(1)}, ...), branch_computations={%region_5.5_spmd, %region_6.6_spmd} | conditional | bytes 6152 | solution.py:295
  347.0 6.4 %branch_1_fun.6 = (bf16[32,8192]{1,0:T(8,128)(2,1)}, bf16[2,4,32,8192]{3,2,1,0:T(8,128)(2,1)}) custom-call(s32[1]{0:T(128)} %bitcast.2.at_ref, s32[768]{0:T(1024)} %reshape.25.idx_ref, bf16[32,8192]{1,0:T(8,128)(2,1)S(1)} %get-tuple-element.423.g_ref, f32[2,4,32,8192]{3,2,1,0:T(8,128)} %get-tuple-element.424.sy_hbm, ...), custom_call_target="tpu_custom_call", output_to_operand_aliasing={{1}: (5, {})} | custom-call | tf_op jit(solution)/shard_map/while/body/eval_jaxpr/cond/branch_1_fun/pallas_call | solution.py:166
  353.4 5.6 %branch_1_fun.7 = (bf16[32,8192]{1,0:T(8,128)(2,1)S(1)}, bf16[2,4,32,8192]{3,2,1,0:T(8,128)(2,1)}) custom-call(s32[1]{0:T(128)} %bitcast.2.at_ref, s32[768]{0:T(1024)} %reshape.25.idx_ref, bf16[32,8192]{1,0:T(8,128)(2,1)} %get-tuple-element.427.g_ref, f32[2,4,32,8192]{3,2,1,0:T(8,128)} %get-tuple-element.424.sy_hbm, ...), custom_call_target="tpu_custom_call", output_to_operand_aliasing={{1}: (5, {})} | custom-call | tf_op jit(solution)/shard_map/while/body/eval_jaxpr/cond/branch_1_fun/pallas_call | solution.py:166
  360.3 9.8 %collective-permute-done.1 = bf16[32,8192]{1,0:T(8,128)(2,1)S(1)} collective-permute-done((bf16[32,8192]{1,0:T(8,128)(2,1)S(1)}, bf16[32,8192]{1,0:T(8,128)(2,1)S(1)}, u32[]{:S(2)}, u32[]{:S(2)}) %collective-permute-start.1) | collective-permute-done | bytes 524320 | tf_op jit(solution)/shard_map/while/body/eval_jaxpr/ppermute | solution.py:27
  370.0 13.5 %shard_map.46 = f32[256,128,128]{2,1,0:T(8,128)} custom-call(s32[768]{0:T(1024)} %reshape.30.idx_ref, bf16[2,4,32,8192]{3,2,1,0:T(8,128)(2,1)} %get-tuple-element.444.h_ref, bf16[2,4,32,8192]{3,2,1,0:T(8,128)(2,1)} %get-tuple-element.446.s_ref), custom_call_target="tpu_custom_call" | custom-call | tf_op jit(solution)/shard_map/pallas_call | solution.py:212
  383.5 6.4 %fusion = bf16[2,2,32,128,128]{4,3,2,1,0:T(8,128)(2,1)} fusion(f32[2,2,2,32,128,128]{5,4,3,2,1,0:T(8,128)} %bitcast.33, s32[]{:T(128)S(6)} %select_n.107), kind=kLoop, calls=%fused_computation.4 | loop fusion | bytes 8388612 | tf_op jit(solution)/shard_map/convert_element_type | solution.py:222
  389.9 7.5 %collective-permute-done.2 = bf16[2,2,32,128,128]{4,3,2,1,0:T(8,128)(2,1)} collective-permute-done((bf16[2,2,32,128,128]{4,3,2,1,0:T(8,128)(2,1)}, bf16[2,2,32,128,128]{4,3,2,1,0:T(8,128)(2,1)}, u32[]{:S(2)}, u32[]{:S(2)}) %collective-permute-start.2) | collective-permute-done | bytes 4194336 | tf_op jit(solution)/shard_map/ppermute | solution.py:222
  397.4 5.9 %bitcast_add_fusion = f32[2,2,32,128,128]{4,3,2,1,0:T(8,128)S(1)} fusion(bf16[2,2,32,128,128]{4,3,2,1,0:T(8,128)(2,1)} %collective-permute-done.2, f32[2,2,2,32,128,128]{5,4,3,2,1,0:T(8,128)} %bitcast.34, s32[]{:T(128)S(6)} %select_n.106), kind=kLoop, calls=%fused_computation.2 | loop fusion | flops 4194304 | bytes 20971524 | tf_op jit(solution)/shard_map/add | solution.py:235
  407.0 26.1 %collective-permute-done.3 = bf16[2,32,128,128]{3,2,1,0:T(8,128)(2,1)} collective-permute-done((bf16[2,32,128,128]{3,2,1,0:T(8,128)(2,1)S(1)}, bf16[2,32,128,128]{3,2,1,0:T(8,128)(2,1)}, u32[]{:S(2)}, u32[]{:S(2)}) %collective-permute-start.3) | collective-permute-done | bytes 2097184 | tf_op jit(solution)/shard_map/ppermute | solution.py:222
  433.1 5.6 %fusion.2 = f32[2,32,128,128]{3,2,1,0:T(8,128)S(1)} fusion(bf16[2,32,128,128]{3,2,1,0:T(8,128)(2,1)} %collective-permute-done.3, f32[2,2,32,128,128]{4,3,2,1,0:T(8,128)} %copy-done, s32[]{:T(128)S(6)} %select_n.112, s32[]{:T(128)S(6)} %select_n.110, pred[]{:T(512)S(6)} %eq.24), kind=kLoop, calls=%fused_computation.8 | loop fusion | flops 3145728 | bytes 14680073 | tf_op jit(solution)/shard_map/add | solution.py:239
  440.9 14.8 %collective-permute-done.4 = bf16[32,128,128]{2,1,0:T(8,128)(2,1)S(1)} collective-permute-done((bf16[32,128,128]{2,1,0:T(8,128)(2,1)S(1)}, bf16[32,128,128]{2,1,0:T(8,128)(2,1)S(1)}, u32[]{:S(2)}, u32[]{:S(2)}) %collective-permute-start.4) | collective-permute-done | bytes 1048608 | tf_op jit(solution)/shard_map/ppermute | solution.py:222
  (58 shorter events, 74.4 us)
Async XLA Ops:
  19.6 13.4 %collective-permute-start = (bf16[32,8192]{1,0:T(8,128)(2,1)S(1)}, bf16[32,8192]{1,0:T(8,128)(2,1)S(1)}, u32[]{:S(2)}, u32[]{:S(2)}) collective-permute-start(bf16[32,8192]{1,0:T(8,128)(2,1)S(1)} %get-tuple-element.625), channel_id=1, source_target_pairs={{0,8},{8,16},{16,24},{1,9},{9,17},{17,25},{2,10},{10,18},{18,26},{... | collective-permute-start | bytes 1572872 | tf_op jit(solution)/shard_map/while/body/eval_jaxpr/ppermute | solution.py:27
  44.3 16.5 %collective-permute-start = (bf16[32,8192]{1,0:T(8,128)(2,1)S(1)}, bf16[32,8192]{1,0:T(8,128)(2,1)S(1)}, u32[]{:S(2)}, u32[]{:S(2)}) collective-permute-start(bf16[32,8192]{1,0:T(8,128)(2,1)S(1)} %get-tuple-element.625), channel_id=1, source_target_pairs={{0,8},{8,16},{16,24},{1,9},{9,17},{17,25},{2,10},{10,18},{18,26},{... | collective-permute-start | bytes 1572872 | tf_op jit(solution)/shard_map/while/body/eval_jaxpr/ppermute | solution.py:27
  72.1 15.8 %collective-permute-start = (bf16[32,8192]{1,0:T(8,128)(2,1)S(1)}, bf16[32,8192]{1,0:T(8,128)(2,1)S(1)}, u32[]{:S(2)}, u32[]{:S(2)}) collective-permute-start(bf16[32,8192]{1,0:T(8,128)(2,1)S(1)} %get-tuple-element.625), channel_id=1, source_target_pairs={{0,8},{8,16},{16,24},{1,9},{9,17},{17,25},{2,10},{10,18},{18,26},{... | collective-permute-start | bytes 1572872 | tf_op jit(solution)/shard_map/while/body/eval_jaxpr/ppermute | solution.py:27
  99.3 14.7 %collective-permute-start = (bf16[32,8192]{1,0:T(8,128)(2,1)S(1)}, bf16[32,8192]{1,0:T(8,128)(2,1)S(1)}, u32[]{:S(2)}, u32[]{:S(2)}) collective-permute-start(bf16[32,8192]{1,0:T(8,128)(2,1)S(1)} %get-tuple-element.625), channel_id=1, source_target_pairs={{0,8},{8,16},{16,24},{1,9},{9,17},{17,25},{2,10},{10,18},{18,26},{... | collective-permute-start | bytes 1572872 | tf_op jit(solution)/shard_map/while/body/eval_jaxpr/ppermute | solution.py:27
  115.1 24.1 %collective-permute-start = (bf16[32,8192]{1,0:T(8,128)(2,1)S(1)}, bf16[32,8192]{1,0:T(8,128)(2,1)S(1)}, u32[]{:S(2)}, u32[]{:S(2)}) collective-permute-start(bf16[32,8192]{1,0:T(8,128)(2,1)S(1)} %get-tuple-element.625), channel_id=1, source_target_pairs={{0,8},{8,16},{16,24},{1,9},{9,17},{17,25},{2,10},{10,18},{18,26},{... | collective-permute-start | bytes 1572872 | tf_op jit(solution)/shard_map/while/body/eval_jaxpr/ppermute | solution.py:27
  140.4 12.0 %collective-permute-start = (bf16[32,8192]{1,0:T(8,128)(2,1)S(1)}, bf16[32,8192]{1,0:T(8,128)(2,1)S(1)}, u32[]{:S(2)}, u32[]{:S(2)}) collective-permute-start(bf16[32,8192]{1,0:T(8,128)(2,1)S(1)} %get-tuple-element.625), channel_id=1, source_target_pairs={{0,8},{8,16},{16,24},{1,9},{9,17},{17,25},{2,10},{10,18},{18,26},{... | collective-permute-start | bytes 1572872 | tf_op jit(solution)/shard_map/while/body/eval_jaxpr/ppermute | solution.py:27
  153.4 19.7 %collective-permute-start = (bf16[32,8192]{1,0:T(8,128)(2,1)S(1)}, bf16[32,8192]{1,0:T(8,128)(2,1)S(1)}, u32[]{:S(2)}, u32[]{:S(2)}) collective-permute-start(bf16[32,8192]{1,0:T(8,128)(2,1)S(1)} %get-tuple-element.625), channel_id=1, source_target_pairs={{0,8},{8,16},{16,24},{1,9},{9,17},{17,25},{2,10},{10,18},{18,26},{... | collective-permute-start | bytes 1572872 | tf_op jit(solution)/shard_map/while/body/eval_jaxpr/ppermute | solution.py:27
  176.8 11.5 %collective-permute-start.1 = (bf16[32,8192]{1,0:T(8,128)(2,1)S(1)}, bf16[32,8192]{1,0:T(8,128)(2,1)S(1)}, u32[]{:S(2)}, u32[]{:S(2)}) collective-permute-start(bf16[32,8192]{1,0:T(8,128)(2,1)S(1)} %get-tuple-element.637), channel_id=1, source_target_pairs={{8,0},{16,8},{24,16},{9,1},{17,9},{25,17},{10,2},{18,10},{26,18},{... | collective-permute-start | bytes 1572872 | tf_op jit(solution)/shard_map/while/body/eval_jaxpr/ppermute | solution.py:27
  189.4 22.6 %collective-permute-start.1 = (bf16[32,8192]{1,0:T(8,128)(2,1)S(1)}, bf16[32,8192]{1,0:T(8,128)(2,1)S(1)}, u32[]{:S(2)}, u32[]{:S(2)}) collective-permute-start(bf16[32,8192]{1,0:T(8,128)(2,1)S(1)} %get-tuple-element.637), channel_id=1, source_target_pairs={{8,0},{16,8},{24,16},{9,1},{17,9},{25,17},{10,2},{18,10},{26,18},{... | collective-permute-start | bytes 1572872 | tf_op jit(solution)/shard_map/while/body/eval_jaxpr/ppermute | solution.py:27
  213.2 51.2 %collective-permute-start.1 = (bf16[32,8192]{1,0:T(8,128)(2,1)S(1)}, bf16[32,8192]{1,0:T(8,128)(2,1)S(1)}, u32[]{:S(2)}, u32[]{:S(2)}) collective-permute-start(bf16[32,8192]{1,0:T(8,128)(2,1)S(1)} %get-tuple-element.637), channel_id=1, source_target_pairs={{8,0},{16,8},{24,16},{9,1},{17,9},{25,17},{10,2},{18,10},{26,18},{... | collective-permute-start | bytes 1572872 | tf_op jit(solution)/shard_map/while/body/eval_jaxpr/ppermute | solution.py:27
  278.2 13.0 %collective-permute-start.1 = (bf16[32,8192]{1,0:T(8,128)(2,1)S(1)}, bf16[32,8192]{1,0:T(8,128)(2,1)S(1)}, u32[]{:S(2)}, u32[]{:S(2)}) collective-permute-start(bf16[32,8192]{1,0:T(8,128)(2,1)S(1)} %get-tuple-element.637), channel_id=1, source_target_pairs={{8,0},{16,8},{24,16},{9,1},{17,9},{25,17},{10,2},{18,10},{26,18},{... | collective-permute-start | bytes 1572872 | tf_op jit(solution)/shard_map/while/body/eval_jaxpr/ppermute | solution.py:27
  305.1 13.0 %collective-permute-start.1 = (bf16[32,8192]{1,0:T(8,128)(2,1)S(1)}, bf16[32,8192]{1,0:T(8,128)(2,1)S(1)}, u32[]{:S(2)}, u32[]{:S(2)}) collective-permute-start(bf16[32,8192]{1,0:T(8,128)(2,1)S(1)} %get-tuple-element.637), channel_id=1, source_target_pairs={{8,0},{16,8},{24,16},{9,1},{17,9},{25,17},{10,2},{18,10},{26,18},{... | collective-permute-start | bytes 1572872 | tf_op jit(solution)/shard_map/while/body/eval_jaxpr/ppermute | solution.py:27
  332.0 13.0 %collective-permute-start.1 = (bf16[32,8192]{1,0:T(8,128)(2,1)S(1)}, bf16[32,8192]{1,0:T(8,128)(2,1)S(1)}, u32[]{:S(2)}, u32[]{:S(2)}) collective-permute-start(bf16[32,8192]{1,0:T(8,128)(2,1)S(1)} %get-tuple-element.637), channel_id=1, source_target_pairs={{8,0},{16,8},{24,16},{9,1},{17,9},{25,17},{10,2},{18,10},{26,18},{... | collective-permute-start | bytes 1572872 | tf_op jit(solution)/shard_map/while/body/eval_jaxpr/ppermute | solution.py:27
  359.0 11.1 %collective-permute-start.1 = (bf16[32,8192]{1,0:T(8,128)(2,1)S(1)}, bf16[32,8192]{1,0:T(8,128)(2,1)S(1)}, u32[]{:S(2)}, u32[]{:S(2)}) collective-permute-start(bf16[32,8192]{1,0:T(8,128)(2,1)S(1)} %get-tuple-element.637), channel_id=1, source_target_pairs={{8,0},{16,8},{24,16},{9,1},{17,9},{25,17},{10,2},{18,10},{26,18},{... | collective-permute-start | bytes 1572872 | tf_op jit(solution)/shard_map/while/body/eval_jaxpr/ppermute | solution.py:27
  389.9 7.5 %collective-permute-start.2 = (bf16[2,2,32,128,128]{4,3,2,1,0:T(8,128)(2,1)}, bf16[2,2,32,128,128]{4,3,2,1,0:T(8,128)(2,1)}, u32[]{:S(2)}, u32[]{:S(2)}) collective-permute-start(bf16[2,2,32,128,128]{4,3,2,1,0:T(8,128)(2,1)} %fusion), channel_id=1, source_target_pairs={{0,1},{1,0},{2,3},{3,2},{4,5},{5,4},{6,7},{7,6},{8,9},{9,8},{10,11... | collective-permute-start | bytes 12582920 | tf_op jit(solution)/shard_map/ppermute | solution.py:222
  403.3 3.2 copy-start
  406.9 26.2 %collective-permute-start.3 = (bf16[2,32,128,128]{3,2,1,0:T(8,128)(2,1)S(1)}, bf16[2,32,128,128]{3,2,1,0:T(8,128)(2,1)}, u32[]{:S(2)}, u32[]{:S(2)}) collective-permute-start(bf16[2,32,128,128]{3,2,1,0:T(8,128)(2,1)S(1)} %fusion.1), channel_id=1, source_target_pairs={{0,2},{1,5},{2,0},{3,7},{4,6},{5,1},{6,4},{7,3},{8,10},{9,13},{10,... | collective-permute-start | bytes 6291464 | tf_op jit(solution)/shard_map/ppermute | solution.py:222
  438.7 2.0 copy-start.1
  440.8 14.9 %collective-permute-start.4 = (bf16[32,128,128]{2,1,0:T(8,128)(2,1)S(1)}, bf16[32,128,128]{2,1,0:T(8,128)(2,1)S(1)}, u32[]{:S(2)}, u32[]{:S(2)}) collective-permute-start(bf16[32,128,128]{2,1,0:T(8,128)(2,1)S(1)} %fusion.3), channel_id=1, source_target_pairs={{0,4},{1,3},{2,6},{3,1},{4,0},{5,7},{6,2},{7,5},{8,12},{9,11},{10,... | collective-permute-start | bytes 3145736 | tf_op jit(solution)/shard_map/ppermute | solution.py:222
where the time goes:
time: 468 us; the launch traced here: 459 us
  waiting for transfers between devices  240 us (51%)
  Pallas kernels  98.9 us (21%)
  starting transfers between devices  59.5 us (13%)
  other arithmetic  30.5 us (7%)
  local copies, waits for them, and re-layouts  28.8 us (6%)
    ppermute x14, waiting for transfers between devices, shifted(): lax.ppermute(value, axis, [(source, source + steps) for source in range(l...  192 us
    ppermute x14, starting transfers between devices, shifted(): lax.ppermute(value, axis, [(source, source + steps) for source in range(l...  59.3 us
    ppermute x3, waiting for transfers between devices, _exchange(): lax.ppermute(send.astype(jnp.bfloat16), 'dp', pairs).astype(jnp.float32)  48.4 us
    pallas_call x8, Pallas kernels, layer_backward(): pl.pallas_call(functools.partial(_bwd_kernel, layer * KMAX, layer), out_s...  47.8 us
    pallas_call x8, Pallas kernels, layer_forward(): pl.pallas_call(functools.partial(_fwd_kernel, layer * KMAX, layer), out_s...  37.5 us
    pallas_call x1, Pallas kernels, segment_dw(): pl.pallas_call(functools.partial(_dw_kernel, mbs), out_shape=jax.ShapeDty...  13.5 us
  transfers between devices with their start and end apart: 17, of which 17 were waited for; matrix products, arithmetic and copies ran while one was open for 0% of the time, Pallas kernels for 0%

commit v1 on v0

--- a/solution.py
+++ b/solution.py
@@ -250,53 +250,50 @@
     x_in = x_in.reshape(mbs, rows_dev, width)
     cotangent = cotangent.reshape(mbs, rows_dev, width)
     idx = block_index.reshape(LSLOT, KMAX, 3)
-    ticks = mbs + segments - 1
-
-    def forward_tick(tick, carry):
-        received, saved_h, saved_y = carry
-        micro = tick - me_segment
-        live = (micro >= 0) & (micro < mbs)
-        place_at = jnp.clip(micro, 0, mbs - 1)
-        first = lax.dynamic_index_in_dim(x_in, place_at, 0, keepdims=False)
-        start = jnp.where(me_segment == 0, first, received)
-
-        def run(operands):
+
+    def tick_body(tick, carry):
+        recv_f, recv_b, saved_h, saved_y, saved_s = carry
+        micro_f = tick - me_segment
+        live_f = (micro_f >= 0) & (micro_f < mbs)
+        at_f = jnp.clip(micro_f, 0, mbs - 1)
+        first = lax.dynamic_index_in_dim(x_in, at_f, 0, keepdims=False)
+        start = jnp.where(me_segment == 0, first, recv_f)
+
+        def run_f(operands):
             h, sh, sy = operands
             for layer in range(LSLOT):
-                h, sh, sy = layer_forward(h, weights, layer, block_index, place_at, sh, sy)
+                h, sh, sy = layer_forward(h, weights, layer, block_index, at_f, sh, sy)
             return (h, sh, sy)
 
-        h_out, saved_h, saved_y = lax.cond(live, run, lambda ops: ops, (start, saved_h, saved_y))
-        received = shifted(h_out, "segment", 1)
-        return (received, saved_h, saved_y)
+        h_out, saved_h, saved_y = lax.cond(live_f, run_f, lambda ops: ops, (start, saved_h, saved_y))
+        send_f = shifted(h_out, "segment", 1)
+
+        micro_b = tick - (2 * segments - 2 - me_segment)
+        live_b = (micro_b >= 0) & (micro_b < mbs)
+        at_b = jnp.clip(micro_b, 0, mbs - 1)
+        top = lax.dynamic_index_in_dim(cotangent, at_b, 0, keepdims=False)
+        grad_in = jnp.where(me_segment == segments - 1, top, recv_b)
+        stash_y_now = saved_y
+
+        def run_b(operands):
+            grad, ss = operands
+            for layer in reversed(range(LSLOT)):
+                grad, ss = layer_backward(grad, stash_y_now, weights, layer, block_index, at_b, ss)
+            return (grad, ss)
+
+        grad_out, saved_s = lax.cond(live_b, run_b, lambda ops: ops, (grad_in, saved_s))
+        send_b = shifted(grad_out, "segment", -1)
+        return (send_f, send_b, saved_h, saved_y, saved_s)
 
     stash_h = jnp.zeros((LSLOT, mbs, rows_dev, width), jnp.bfloat16)
     stash_y = jnp.zeros((LSLOT, mbs, rows_dev, width), jnp.float32)
+    stash_s = jnp.zeros((LSLOT, mbs, rows_dev, width), jnp.bfloat16)
     blank = jnp.zeros((rows_dev, width), jnp.bfloat16)
-    unused_recv, stash_h, stash_y = lax.fori_loop(
-        0, ticks, forward_tick, (blank, stash_h, stash_y)
-    )
-    stash_s = jnp.zeros((LSLOT, mbs, rows_dev, width), jnp.bfloat16)
-
-    def backward_tick(tick, carry):
-        received, saved_s = carry
-        micro = tick - (segments - 1 - me_segment)
-        live = (micro >= 0) & (micro < mbs)
-        place_at = jnp.clip(micro, 0, mbs - 1)
-        top = lax.dynamic_index_in_dim(cotangent, place_at, 0, keepdims=False)
-        grad_in = jnp.where(me_segment == segments - 1, top, received)
-
-        def run(operands):
-            grad, ss = operands
-            for layer in reversed(range(LSLOT)):
-                grad, ss = layer_backward(grad, stash_y, weights, layer, block_index, place_at, ss)
-            return (grad, ss)
-
-        grad_out, saved_s = lax.cond(live, run, lambda ops: ops, (grad_in, saved_s))
-        received = shifted(grad_out, "segment", -1)
-        return (received, saved_s)
-
-    unused_grad, stash_s = lax.fori_loop(0, ticks, backward_tick, (blank, stash_s))
+    ticks = mbs + 2 * segments - 2
+    carry = (blank, blank, stash_h, stash_y, stash_s)
+    for tick in range(ticks):
+        carry = tick_body(tick, carry)
+    unused_f, unused_b, stash_h, stash_y, stash_s = carry
     acc = segment_dw(stash_h, stash_s, block_index, mbs)
     return dp_reduce_scatter(acc)
 

time: 468 us -> 421 us (0.90); the launches traced: 459 us -> 417 us
  waiting for transfers between devices: 240 us -> 123 us
  starting transfers between devices: 59.5 us -> 111 us
  Pallas kernels: 98.9 us -> 115 us
  local copies, waits for them, and re-layouts: 28.8 us -> 35 us
    ppermute x14 -> x18, waiting for transfers between devices: 192 us -> 74.5 us  [shifted(): lax.ppermute(value, axis, [(source, source + steps) for source in range(l...]
    ppermute x14 -> x18, starting transfers between devices: 59.3 us -> 111 us  [shifted(): lax.ppermute(value, axis, [(source, source + steps) for source in range(l...]
    pallas_call x8, Pallas kernels: 47.8 us -> 58 us  [layer_backward(): pl.pallas_call(functools.partial(_bwd_kernel, layer * KMAX, layer), out_s...]
    another operation x2 -> x10, local copies, waits for them, and re-layouts: 4.89 us -> 10.8 us
    select_n x14 -> x19, other arithmetic: 15.4 us -> 15.4 us  [the longest x10 13.8 us: tick_body(): grad_in = jnp.where(me_segment == segments - 1, top, recv_b)]
  transfers between devices with their start and end apart: 17 -> 21, of which waited for: 17 -> 13; matrix products, arithmetic and copies ran while one was open for 0% -> 6% of each run, Pallas kernels for 0% -> 18%
where the time goes in v1:
time: 421 us; the launch traced here: 417 us
  waiting for transfers between devices  123 us (29%)
  Pallas kernels  115 us (27%)
  starting transfers between devices  111 us (26%)
  local copies, waits for them, and re-layouts  35 us (8%)
  other arithmetic  30.5 us (7%)
    ppermute x18, starting transfers between devices, shifted(): lax.ppermute(value, axis, [(source, source + steps) for source in range(l...  111 us
    ppermute x18, waiting for transfers between devices, shifted(): lax.ppermute(value, axis, [(source, source + steps) for source in range(l...  74.5 us
    pallas_call x8, Pallas kernels, layer_backward(): pl.pallas_call(functools.partial(_bwd_kernel, layer * KMAX, layer), out_s...  58 us
    ppermute x3, waiting for transfers between devices, _exchange(): lax.ppermute(send.astype(jnp.bfloat16), 'dp', pairs).astype(jnp.float32)  48.4 us
    pallas_call x8, Pallas kernels, layer_forward(): pl.pallas_call(functools.partial(_fwd_kernel, layer * KMAX, layer), out_s...  41.7 us
    pallas_call x1, Pallas kernels, segment_dw(): pl.pallas_call(functools.partial(_dw_kernel, mbs), out_shape=jax.ShapeDty...  15.6 us
    select_n x10, other arithmetic, tick_body(): grad_in = jnp.where(me_segment == segments - 1, top, recv_b)  13.8 us
    another operation x10, local copies, waits for them, and re-layouts  10.8 us
  transfers between devices with their start and end apart: 21, of which 13 were waited for; matrix products, arithmetic and copies ran while one was open for 6% of the time, Pallas kernels for 18%

profile of v1, /device:TPU:0, one launch (start us, length us, event | category | flops | bytes accessed | tf_op | source)
XLA Modules:
  0.0 417.3 jit_solution(6602881236922443249)
XLA Ops:
  1.1 18.8 %conditional.20 = ((bf16[32,8192]{1,0:T(8,128)(2,1)S(1)}, bf16[2,4,32,8192]{3,2,1,0:T(8,128)(2,1)}, f32[2,4,32,8192]{3,2,1,0:T(8,128)})) conditional(s32[]{:T(128)} %convert_element_type.93, bf16[32,8192]{1,0:T(8,128)(2,1)S(1)} %select_bitcast_fusion.1, (s32[]{:T(128)}, s32[256,3]{0,1:T(4,128)}, bf16[32,8192]{1,0:T(8,128)(2,1)S(1)}, ...), branch_computations={%region_0.1_spmd, %region_1.2_spmd} | conditional | bytes 12595214 | solution.py:268
  9.5 4.9 %branch_1_fun.48 = (bf16[32,8192]{1,0:T(8,128)(2,1)}, bf16[2,4,32,8192]{3,2,1,0:T(8,128)(2,1)}, f32[2,4,32,8192]{3,2,1,0:T(8,128)}) custom-call(s32[1]{0:T(128)} %bitcast.at_ref, s32[768]{0:T(1024)} %reshape.101.idx_ref, bf16[32,8192]{1,0:T(8,128)(2,1)S(1)} %get-tuple-element.422.h_ref, ...), custom_call_target="tpu_custom_call", output_to_operand_aliasing={{1}: (4, {}), {2}: (5, {})} | custom-call | tf_op jit(solution)/shard_map/cond/branch_1_fun/pallas_call | solution.py:99
  14.4 5.5 %branch_1_fun.49 = (bf16[32,8192]{1,0:T(8,128)(2,1)S(1)}, bf16[2,4,32,8192]{3,2,1,0:T(8,128)(2,1)}, f32[2,4,32,8192]{3,2,1,0:T(8,128)}) custom-call(s32[1]{0:T(128)} %bitcast.at_ref, s32[768]{0:T(1024)} %reshape.101.idx_ref, bf16[32,8192]{1,0:T(8,128)(2,1)} %get-tuple-element.424.h_ref, ...), custom_call_target="tpu_custom_call", output_to_operand_aliasing={{1}: (4, {}), {2}: (5, {})} | custom-call | tf_op jit(solution)/shard_map/cond/branch_1_fun/pallas_call | solution.py:99
  26.9 6.3 %collective-permute-done = bf16[32,8192]{1,0:T(8,128)(2,1)} collective-permute-done((bf16[32,8192]{1,0:T(8,128)(2,1)S(1)}, bf16[32,8192]{1,0:T(8,128)(2,1)}, u32[]{:S(2)}, u32[]{:S(2)}) %collective-permute-start) | collective-permute-done | bytes 524320 | tf_op jit(solution)/shard_map/ppermute | solution.py:27
  33.3 12.0 %conditional.21 = ((bf16[32,8192]{1,0:T(8,128)(2,1)S(1)}, bf16[2,4,32,8192]{3,2,1,0:T(8,128)(2,1)}, f32[2,4,32,8192]{3,2,1,0:T(8,128)})) conditional(s32[]{:T(128)} %convert_element_type.92, (bf16[32,8192]{1,0:T(8,128)(2,1)S(1)}, bf16[2,4,32,8192]{3,2,1,0:T(8,128)(2,1)}, f32[2,4,32,8192]{3,2,1,0:T(8,128)}) %tuple.143, (s32[]{:T(128)}, ...), branch_computations={%region_2.3_spmd, %region_3.4_spmd} | conditional | bytes 12296 | solution.py:268
  34.9 4.9 %branch_1_fun.50 = (bf16[32,8192]{1,0:T(8,128)(2,1)}, bf16[2,4,32,8192]{3,2,1,0:T(8,128)(2,1)}, f32[2,4,32,8192]{3,2,1,0:T(8,128)}) custom-call(s32[1]{0:T(128)} %bitcast.1.at_ref, s32[768]{0:T(1024)} %reshape.107.idx_ref, bf16[32,8192]{1,0:T(8,128)(2,1)S(1)} %get-tuple-element.429.h_ref, ...), custom_call_target="tpu_custom_call", output_to_operand_aliasing={{1}: (4, {}), {2}: (5, {})} | custom-call | tf_op jit(solution)/shard_map/cond/branch_1_fun/pallas_call | solution.py:99
  39.9 5.4 %branch_1_fun.51 = (bf16[32,8192]{1,0:T(8,128)(2,1)S(1)}, bf16[2,4,32,8192]{3,2,1,0:T(8,128)(2,1)}, f32[2,4,32,8192]{3,2,1,0:T(8,128)}) custom-call(s32[1]{0:T(128)} %bitcast.1.at_ref, s32[768]{0:T(1024)} %reshape.107.idx_ref, bf16[32,8192]{1,0:T(8,128)(2,1)} %get-tuple-element.433.h_ref, ...), custom_call_target="tpu_custom_call", output_to_operand_aliasing={{1}: (4, {}), {2}: (5, {})} | custom-call | tf_op jit(solution)/shard_map/cond/branch_1_fun/pallas_call | solution.py:99
  45.3 5.4 %collective-permute-start.1 = (bf16[32,8192]{1,0:T(8,128)(2,1)S(1)}, bf16[32,8192]{1,0:T(8,128)(2,1)}, u32[]{:S(2)}, u32[]{:S(2)}) collective-permute-start(bf16[32,8192]{1,0:T(8,128)(2,1)S(1)} %get-tuple-element.649), channel_id=1, source_target_pairs={{0,8},{8,16},{16,24},{1,9},{9,17},{17,25},{2,10},{10,18},{18,26},{... | collective-permute-start | bytes 1572872 | tf_op jit(solution)/shard_map/ppermute | solution.py:27
  53.2 7.8 %collective-permute-done.1 = bf16[32,8192]{1,0:T(8,128)(2,1)} collective-permute-done((bf16[32,8192]{1,0:T(8,128)(2,1)S(1)}, bf16[32,8192]{1,0:T(8,128)(2,1)}, u32[]{:S(2)}, u32[]{:S(2)}) %collective-permute-start.1) | collective-permute-done | bytes 524320 | tf_op jit(solution)/shard_map/ppermute | solution.py:27
  61.1 13.4 %conditional.22 = ((bf16[32,8192]{1,0:T(8,128)(2,1)S(1)}, bf16[2,4,32,8192]{3,2,1,0:T(8,128)(2,1)}, f32[2,4,32,8192]{3,2,1,0:T(8,128)})) conditional(s32[]{:T(128)} %convert_element_type.91, (bf16[32,8192]{1,0:T(8,128)(2,1)S(1)}, bf16[2,4,32,8192]{3,2,1,0:T(8,128)(2,1)}, f32[2,4,32,8192]{3,2,1,0:T(8,128)}) %tuple.145, (s32[]{:T(128)}, ...), branch_computations={%region_4.5_spmd, %region_5.6_spmd} | conditional | bytes 12296 | solution.py:268
  62.8 5.1 %branch_1_fun.52 = (bf16[32,8192]{1,0:T(8,128)(2,1)}, bf16[2,4,32,8192]{3,2,1,0:T(8,128)(2,1)}, f32[2,4,32,8192]{3,2,1,0:T(8,128)}) custom-call(s32[1]{0:T(128)} %bitcast.2.at_ref, s32[768]{0:T(1024)} %reshape.109.idx_ref, bf16[32,8192]{1,0:T(8,128)(2,1)S(1)} %get-tuple-element.438.h_ref, ...), custom_call_target="tpu_custom_call", output_to_operand_aliasing={{1}: (4, {}), {2}: (5, {})} | custom-call | tf_op jit(solution)/shard_map/cond/branch_1_fun/pallas_call | solution.py:99
  67.9 5.6 %branch_1_fun.53 = (bf16[32,8192]{1,0:T(8,128)(2,1)S(1)}, bf16[2,4,32,8192]{3,2,1,0:T(8,128)(2,1)}, f32[2,4,32,8192]{3,2,1,0:T(8,128)}) custom-call(s32[1]{0:T(128)} %bitcast.2.at_ref, s32[768]{0:T(1024)} %reshape.109.idx_ref, bf16[32,8192]{1,0:T(8,128)(2,1)} %get-tuple-element.442.h_ref, ...), custom_call_target="tpu_custom_call", output_to_operand_aliasing={{1}: (4, {}), {2}: (5, {})} | custom-call | tf_op jit(solution)/shard_map/cond/branch_1_fun/pallas_call | solution.py:99
  74.5 6.4 %collective-permute-start.2 = (bf16[32,8192]{1,0:T(8,128)(2,1)S(1)}, bf16[32,8192]{1,0:T(8,128)(2,1)}, u32[]{:S(2)}, u32[]{:S(2)}) collective-permute-start(bf16[32,8192]{1,0:T(8,128)(2,1)S(1)} %get-tuple-element.652), channel_id=1, source_target_pairs={{0,8},{8,16},{16,24},{1,9},{9,17},{17,25},{2,10},{10,18},{18,26},{... | collective-permute-start | bytes 1572872 | tf_op jit(solution)/shard_map/ppermute | solution.py:27
  83.5 6.9 %collective-permute-done.2 = bf16[32,8192]{1,0:T(8,128)(2,1)} collective-permute-done((bf16[32,8192]{1,0:T(8,128)(2,1)S(1)}, bf16[32,8192]{1,0:T(8,128)(2,1)}, u32[]{:S(2)}, u32[]{:S(2)}) %collective-permute-start.2) | collective-permute-done | bytes 524320 | tf_op jit(solution)/shard_map/ppermute | solution.py:27
  90.5 12.0 %conditional.23 = ((bf16[32,8192]{1,0:T(8,128)(2,1)S(1)}, bf16[2,4,32,8192]{3,2,1,0:T(8,128)(2,1)}, f32[2,4,32,8192]{3,2,1,0:T(8,128)})) conditional(s32[]{:T(128)} %convert_element_type.90, (bf16[32,8192]{1,0:T(8,128)(2,1)S(1)}, bf16[2,4,32,8192]{3,2,1,0:T(8,128)(2,1)}, f32[2,4,32,8192]{3,2,1,0:T(8,128)}) %tuple.147, (s32[]{:T(128)}, ...), branch_computations={%region_6.7_spmd, %region_7.8_spmd} | conditional | bytes 12296 | solution.py:268
  92.1 4.9 %branch_1_fun.54 = (bf16[32,8192]{1,0:T(8,128)(2,1)}, bf16[2,4,32,8192]{3,2,1,0:T(8,128)(2,1)}, f32[2,4,32,8192]{3,2,1,0:T(8,128)}) custom-call(s32[1]{0:T(128)} %bitcast.3.at_ref, s32[768]{0:T(1024)} %reshape.115.idx_ref, bf16[32,8192]{1,0:T(8,128)(2,1)S(1)} %get-tuple-element.447.h_ref, ...), custom_call_target="tpu_custom_call", output_to_operand_aliasing={{1}: (4, {}), {2}: (5, {})} | custom-call | tf_op jit(solution)/shard_map/cond/branch_1_fun/pallas_call | solution.py:99
  97.1 5.4 %branch_1_fun.55 = (bf16[32,8192]{1,0:T(8,128)(2,1)S(1)}, bf16[2,4,32,8192]{3,2,1,0:T(8,128)(2,1)}, f32[2,4,32,8192]{3,2,1,0:T(8,128)}) custom-call(s32[1]{0:T(128)} %bitcast.3.at_ref, s32[768]{0:T(1024)} %reshape.115.idx_ref, bf16[32,8192]{1,0:T(8,128)(2,1)} %get-tuple-element.451.h_ref, ...), custom_call_target="tpu_custom_call", output_to_operand_aliasing={{1}: (4, {}), {2}: (5, {})} | custom-call | tf_op jit(solution)/shard_map/cond/branch_1_fun/pallas_call | solution.py:99
  102.5 5.5 %collective-permute-start.3 = (bf16[32,8192]{1,0:T(8,128)(2,1)S(1)}, bf16[32,8192]{1,0:T(8,128)(2,1)}, u32[]{:S(2)}, u32[]{:S(2)}) collective-permute-start(bf16[32,8192]{1,0:T(8,128)(2,1)S(1)} %get-tuple-element.655), channel_id=1, source_target_pairs={{0,8},{8,16},{16,24},{1,9},{9,17},{17,25},{2,10},{10,18},{18,26},{... | collective-permute-start | bytes 1572872 | tf_op jit(solution)/shard_map/ppermute | solution.py:27
  110.5 6.0 %collective-permute-done.3 = bf16[32,8192]{1,0:T(8,128)(2,1)} collective-permute-done((bf16[32,8192]{1,0:T(8,128)(2,1)S(1)}, bf16[32,8192]{1,0:T(8,128)(2,1)}, u32[]{:S(2)}, u32[]{:S(2)}) %collective-permute-start.3) | collective-permute-done | bytes 524320 | tf_op jit(solution)/shard_map/ppermute | solution.py:27
  116.8 17.4 %collective-permute-start.4 = (bf16[32,8192]{1,0:T(8,128)(2,1)S(1)}, bf16[32,8192]{1,0:T(8,128)(2,1)}, u32[]{:S(2)}, u32[]{:S(2)}) collective-permute-start(bf16[32,8192]{1,0:T(8,128)(2,1)S(1)} %get-tuple-element.658), channel_id=1, source_target_pairs={{0,8},{8,16},{16,24},{1,9},{9,17},{17,25},{2,10},{10,18},{18,26},{... | collective-permute-start | bytes 1572872 | tf_op jit(solution)/shard_map/ppermute | solution.py:27
  136.8 5.1 %collective-permute-done.4 = bf16[32,8192]{1,0:T(8,128)(2,1)} collective-permute-done((bf16[32,8192]{1,0:T(8,128)(2,1)S(1)}, bf16[32,8192]{1,0:T(8,128)(2,1)}, u32[]{:S(2)}, u32[]{:S(2)}) %collective-permute-start.4) | collective-permute-done | bytes 524320 | tf_op jit(solution)/shard_map/ppermute | solution.py:27
  142.0 7.9 %collective-permute-start.5 = (bf16[32,8192]{1,0:T(8,128)(2,1)S(1)}, bf16[32,8192]{1,0:T(8,128)(2,1)}, u32[]{:S(2)}, u32[]{:S(2)}) collective-permute-start(bf16[32,8192]{1,0:T(8,128)(2,1)S(1)} %get-tuple-element.661), channel_id=1, source_target_pairs={{0,8},{8,16},{16,24},{1,9},{9,17},{17,25},{2,10},{10,18},{18,26},{... | collective-permute-start | bytes 1572872 | tf_op jit(solution)/shard_map/ppermute | solution.py:27
  157.0 40.5 %collective-permute-start.6 = (bf16[32,8192]{1,0:T(8,128)(2,1)S(1)}, bf16[32,8192]{1,0:T(8,128)(2,1)}, u32[]{:S(2)}, u32[]{:S(2)}) collective-permute-start(bf16[32,8192]{1,0:T(8,128)(2,1)S(1)} %get-tuple-element.664), channel_id=1, source_target_pairs={{0,8},{8,16},{16,24},{1,9},{9,17},{17,25},{2,10},{10,18},{18,26},{... | collective-permute-start | bytes 1572872 | tf_op jit(solution)/shard_map/ppermute | solution.py:27
  197.5 6.4 %collective-permute-done.14 = bf16[32,8192]{1,0:T(8,128)(2,1)} collective-permute-done((bf16[32,8192]{1,0:T(8,128)(2,1)S(1)}, bf16[32,8192]{1,0:T(8,128)(2,1)}, u32[]{:S(2)}, u32[]{:S(2)}) %collective-permute-start.14) | collective-permute-done | bytes 524320 | tf_op jit(solution)/shard_map/ppermute | solution.py:27
  205.2 15.6 %conditional.36 = ((bf16[32,8192]{1,0:T(8,128)(2,1)S(1)}, bf16[2,4,32,8192]{3,2,1,0:T(8,128)(2,1)})) conditional(s32[]{:T(128)} %convert_element_type.97, (bf16[32,8192]{1,0:T(8,128)(2,1)S(1)}, bf16[2,4,32,8192]{3,2,1,0:T(8,128)(2,1)}) %tuple.172, (s32[]{:T(128)}, s32[256,3]{0,1:T(4,128)}, bf16[32,8192]{1,0:T(8,128)(2,1)S(1)}, ...), branch_computations={%region_32.33_spmd, %region_33.34_spmd} | conditional | bytes 12296 | solution.py:284
  206.9 8.0 %branch_1_fun.80 = (bf16[32,8192]{1,0:T(8,128)(2,1)}, bf16[2,4,32,8192]{3,2,1,0:T(8,128)(2,1)}) custom-call(s32[1]{0:T(128)} %bitcast.17.at_ref, s32[768]{0:T(1024)} %reshape.169.idx_ref, bf16[32,8192]{1,0:T(8,128)(2,1)S(1)} %get-tuple-element.561.g_ref, f32[2,4,32,8192]{3,2,1,0:T(8,128)} %get-tuple-element.562.sy_hbm, ...), custom_call_target="tpu_custom_call", output_to_operand_aliasing={{1}: (5, {})} | custom-call | tf_op jit(solution)/shard_map/cond/branch_1_fun/pallas_call | solution.py:166
  214.8 6.0 %branch_1_fun.81 = (bf16[32,8192]{1,0:T(8,128)(2,1)S(1)}, bf16[2,4,32,8192]{3,2,1,0:T(8,128)(2,1)}) custom-call(s32[1]{0:T(128)} %bitcast.17.at_ref, s32[768]{0:T(1024)} %reshape.169.idx_ref, bf16[32,8192]{1,0:T(8,128)(2,1)} %get-tuple-element.565.g_ref, f32[2,4,32,8192]{3,2,1,0:T(8,128)} %get-tuple-element.562.sy_hbm, ...), custom_call_target="tpu_custom_call", output_to_operand_aliasing={{1}: (5, {})} | custom-call | tf_op jit(solution)/shard_map/cond/branch_1_fun/pallas_call | solution.py:166
  222.2 7.0 %collective-permute-start.7 = (bf16[32,8192]{1,0:T(8,128)(2,1)S(1)}, bf16[32,8192]{1,0:T(8,128)(2,1)}, u32[]{:S(2)}, u32[]{:S(2)}) collective-permute-start(bf16[32,8192]{1,0:T(8,128)(2,1)S(1)} %get-tuple-element.667), channel_id=1, source_target_pairs={{0,8},{8,16},{16,24},{1,9},{9,17},{17,25},{2,10},{10,18},{18,26},{... | collective-permute-start | bytes 1572872 | tf_op jit(solution)/shard_map/ppermute | solution.py:27
  229.2 5.5 %collective-permute-done.15 = bf16[32,8192]{1,0:T(8,128)(2,1)} collective-permute-done((bf16[32,8192]{1,0:T(8,128)(2,1)S(1)}, bf16[32,8192]{1,0:T(8,128)(2,1)}, u32[]{:S(2)}, u32[]{:S(2)}) %collective-permute-start.15) | collective-permute-done | bytes 524320 | tf_op jit(solution)/shard_map/ppermute | solution.py:27
  236.8 16.9 %conditional.37 = ((bf16[32,8192]{1,0:T(8,128)(2,1)}, bf16[2,4,32,8192]{3,2,1,0:T(8,128)(2,1)})) conditional(s32[]{:T(128)} %convert_element_type.96, (bf16[32,8192]{1,0:T(8,128)(2,1)}, bf16[2,4,32,8192]{3,2,1,0:T(8,128)(2,1)}) %tuple.174, (s32[]{:T(128)}, s32[256,3]{0,1:T(4,128)}, bf16[32,8192]{1,0:T(8,128)(2,1)}, f32[2,4,32,8192]{3,2,1,0:T(8,128)}, ...), branch_computations={%region_34.35_spmd, %region_35.36_spmd} | conditional | bytes 12296 | solution.py:284
  238.4 8.3 %branch_1_fun.82 = (bf16[32,8192]{1,0:T(8,128)(2,1)}, bf16[2,4,32,8192]{3,2,1,0:T(8,128)(2,1)}) custom-call(s32[1]{0:T(128)} %bitcast.18.at_ref, s32[768]{0:T(1024)} %reshape.171.idx_ref, bf16[32,8192]{1,0:T(8,128)(2,1)} %get-tuple-element.569.g_ref, f32[2,4,32,8192]{3,2,1,0:T(8,128)} %get-tuple-element.570.sy_hbm, ...), custom_call_target="tpu_custom_call", output_to_operand_aliasing={{1}: (5, {})} | custom-call | tf_op jit(solution)/shard_map/cond/branch_1_fun/pallas_call | solution.py:166
  246.7 6.8 %branch_1_fun.83 = (bf16[32,8192]{1,0:T(8,128)(2,1)}, bf16[2,4,32,8192]{3,2,1,0:T(8,128)(2,1)}) custom-call(s32[1]{0:T(128)} %bitcast.18.at_ref, s32[768]{0:T(1024)} %reshape.171.idx_ref, bf16[32,8192]{1,0:T(8,128)(2,1)} %get-tuple-element.573.g_ref, f32[2,4,32,8192]{3,2,1,0:T(8,128)} %get-tuple-element.570.sy_hbm, ...), custom_call_target="tpu_custom_call", output_to_operand_aliasing={{1}: (5, {})} | custom-call | tf_op jit(solution)/shard_map/cond/branch_1_fun/pallas_call | solution.py:166
  255.0 17.9 %collective-permute-done.16 = bf16[32,8192]{1,0:T(8,128)(2,1)S(1)} collective-permute-done((bf16[32,8192]{1,0:T(8,128)(2,1)}, bf16[32,8192]{1,0:T(8,128)(2,1)S(1)}, u32[]{:S(2)}, u32[]{:S(2)}) %collective-permute-start.16) | collective-permute-done | bytes 524320 | tf_op jit(solution)/shard_map/ppermute | solution.py:27
  274.0 6.9 %collective-permute-start.8 = (bf16[32,8192]{1,0:T(8,128)(2,1)S(1)}, bf16[32,8192]{1,0:T(8,128)(2,1)}, u32[]{:S(2)}, u32[]{:S(2)}) collective-permute-start(bf16[32,8192]{1,0:T(8,128)(2,1)S(1)} %get-tuple-element.672), channel_id=1, source_target_pairs={{0,8},{8,16},{16,24},{1,9},{9,17},{17,25},{2,10},{10,18},{18,26},{... | collective-permute-start | bytes 1572872 | tf_op jit(solution)/shard_map/ppermute | solution.py:27
  281.0 15.6 %conditional.38 = ((bf16[32,8192]{1,0:T(8,128)(2,1)S(1)}, bf16[2,4,32,8192]{3,2,1,0:T(8,128)(2,1)})) conditional(s32[]{:T(128)} %convert_element_type.95, (bf16[32,8192]{1,0:T(8,128)(2,1)S(1)}, bf16[2,4,32,8192]{3,2,1,0:T(8,128)(2,1)}) %tuple.176, (s32[]{:T(128)}, s32[256,3]{0,1:T(4,128)}, bf16[32,8192]{1,0:T(8,128)(2,1)S(1)}, ...), branch_computations={%region_36.37_spmd.clone, %region_37.38_spmd.clone} | conditional | bytes 12296 | solution.py:284
  282.6 8.0 %branch_1_fun.86 = (bf16[32,8192]{1,0:T(8,128)(2,1)}, bf16[2,4,32,8192]{3,2,1,0:T(8,128)(2,1)}) custom-call(s32[1]{0:T(128)} %bitcast.50.at_ref, s32[768]{0:T(1024)} %reshape.185.idx_ref, bf16[32,8192]{1,0:T(8,128)(2,1)S(1)} %get-tuple-element.700.g_ref, f32[2,4,32,8192]{3,2,1,0:T(8,128)} %get-tuple-element.701.sy_hbm, ...), custom_call_target="tpu_custom_call", output_to_operand_aliasing={{1}: (5, {})} | custom-call | tf_op jit(solution)/shard_map/cond/branch_1_fun/pallas_call | solution.py:166
  290.5 6.0 %branch_1_fun.87 = (bf16[32,8192]{1,0:T(8,128)(2,1)S(1)}, bf16[2,4,32,8192]{3,2,1,0:T(8,128)(2,1)}) custom-call(s32[1]{0:T(128)} %bitcast.50.at_ref, s32[768]{0:T(1024)} %reshape.185.idx_ref, bf16[32,8192]{1,0:T(8,128)(2,1)} %get-tuple-element.704.g_ref, f32[2,4,32,8192]{3,2,1,0:T(8,128)} %get-tuple-element.701.sy_hbm, ...), custom_call_target="tpu_custom_call", output_to_operand_aliasing={{1}: (5, {})} | custom-call | tf_op jit(solution)/shard_map/cond/branch_1_fun/pallas_call | solution.py:166
  299.5 8.3 %collective-permute-done.17 = bf16[32,8192]{1,0:T(8,128)(2,1)} collective-permute-done((bf16[32,8192]{1,0:T(8,128)(2,1)S(1)}, bf16[32,8192]{1,0:T(8,128)(2,1)}, u32[]{:S(2)}, u32[]{:S(2)}) %collective-permute-start.17) | collective-permute-done | bytes 524320 | tf_op jit(solution)/shard_map/ppermute | solution.py:27
  307.8 18.1 %conditional.39 = (bf16[2,4,32,8192]{3,2,1,0:T(8,128)(2,1)}) conditional(s32[]{:T(128)} %convert_element_type.94, bf16[2,4,32,8192]{3,2,1,0:T(8,128)(2,1)} %get-tuple-element.690, (s32[]{:T(128)}, s32[256,3]{0,1:T(4,128)S(1)}, pred[]{:T(512)}, bf16[4,32,8192]{2,1,0:T(8,128)(2,1)}, bf16[32,8192]{1,0:T(8,128)(2,1)}, ...), branch_computations={%region_38.39_spmd, %region_39.40_spmd} | conditional | flops 262146 | bytes 1585189 | solution.py:284
  310.8 8.3 %branch_1_fun.84 = (bf16[32,8192]{1,0:T(8,128)(2,1)}, bf16[2,4,32,8192]{3,2,1,0:T(8,128)(2,1)}) custom-call(s32[1]{0:T(128)} %bitcast.19.at_ref, s32[768]{0:T(1024)} %reshape.175.idx_ref, bf16[32,8192]{1,0:T(8,128)(2,1)} %bitcast_select_fusion.1.g_ref, f32[2,4,32,8192]{3,2,1,0:T(8,128)} %get-tuple-element.592.sy_hbm, ...), custom_call_target="tpu_custom_call", output_to_operand_aliasing={{1}: (5, {})} | custom-call | tf_op jit(solution)/shard_map/cond/branch_1_fun/pallas_call | solution.py:166
  319.1 6.8 %branch_1_fun.85 = (bf16[32,8192]{1,0:T(8,128)(2,1)}, bf16[2,4,32,8192]{3,2,1,0:T(8,128)(2,1)}) custom-call(s32[1]{0:T(128)} %bitcast.19.at_ref, s32[768]{0:T(1024)} %reshape.175.idx_ref, bf16[32,8192]{1,0:T(8,128)(2,1)} %get-tuple-element.595.g_ref, f32[2,4,32,8192]{3,2,1,0:T(8,128)} %get-tuple-element.592.sy_hbm, ...), custom_call_target="tpu_custom_call", output_to_operand_aliasing={{1}: (5, {})} | custom-call | tf_op jit(solution)/shard_map/cond/branch_1_fun/pallas_call | solution.py:166
  325.9 15.6 %shard_map.46 = f32[256,128,128]{2,1,0:T(8,128)} custom-call(s32[768]{0:T(1024)} %reshape.180.idx_ref, bf16[2,4,32,8192]{3,2,1,0:T(8,128)(2,1)} %get-tuple-element.673.h_ref, bf16[2,4,32,8192]{3,2,1,0:T(8,128)(2,1)} %get-tuple-element.944.s_ref), custom_call_target="tpu_custom_call" | custom-call | tf_op jit(solution)/shard_map/pallas_call | solution.py:212
  341.5 6.4 %fusion = bf16[2,2,32,128,128]{4,3,2,1,0:T(8,128)(2,1)} fusion(f32[2,2,2,32,128,128]{5,4,3,2,1,0:T(8,128)} %bitcast.83, s32[]{:T(128)S(6)} %select_n.223), kind=kLoop, calls=%fused_computation.4 | loop fusion | bytes 8388612 | tf_op jit(solution)/shard_map/convert_element_type | solution.py:222
  347.9 7.5 %collective-permute-done.18 = bf16[2,2,32,128,128]{4,3,2,1,0:T(8,128)(2,1)} collective-permute-done((bf16[2,2,32,128,128]{4,3,2,1,0:T(8,128)(2,1)}, bf16[2,2,32,128,128]{4,3,2,1,0:T(8,128)(2,1)}, u32[]{:S(2)}, u32[]{:S(2)}) %collective-permute-start.18) | collective-permute-done | bytes 4194336 | tf_op jit(solution)/shard_map/ppermute | solution.py:222
  355.4 5.9 %bitcast_add_fusion = f32[2,2,32,128,128]{4,3,2,1,0:T(8,128)S(1)} fusion(bf16[2,2,32,128,128]{4,3,2,1,0:T(8,128)(2,1)} %collective-permute-done.18, f32[2,2,2,32,128,128]{5,4,3,2,1,0:T(8,128)} %bitcast.84, s32[]{:T(128)S(6)} %select_n.222), kind=kLoop, calls=%fused_computation.2 | loop fusion | flops 4194304 | bytes 20971524 | tf_op jit(solution)/shard_map/add | solution.py:235
  365.1 26.1 %collective-permute-done.19 = bf16[2,32,128,128]{3,2,1,0:T(8,128)(2,1)} collective-permute-done((bf16[2,32,128,128]{3,2,1,0:T(8,128)(2,1)S(1)}, bf16[2,32,128,128]{3,2,1,0:T(8,128)(2,1)}, u32[]{:S(2)}, u32[]{:S(2)}) %collective-permute-start.19) | collective-permute-done | bytes 2097184 | tf_op jit(solution)/shard_map/ppermute | solution.py:222
  391.2 5.6 %fusion.2 = f32[2,32,128,128]{3,2,1,0:T(8,128)S(1)} fusion(bf16[2,32,128,128]{3,2,1,0:T(8,128)(2,1)} %collective-permute-done.19, f32[2,2,32,128,128]{4,3,2,1,0:T(8,128)} %copy-done, s32[]{:T(128)S(6)} %select_n.228, s32[]{:T(128)S(6)} %select_n.226, pred[]{:T(512)S(6)} %eq.8), kind=kLoop, calls=%fused_computation.8 | loop fusion | flops 3145728 | bytes 14680073 | tf_op jit(solution)/shard_map/add | solution.py:239
  399.0 14.8 %collective-permute-done.20 = bf16[32,128,128]{2,1,0:T(8,128)(2,1)S(1)} collective-permute-done((bf16[32,128,128]{2,1,0:T(8,128)(2,1)S(1)}, bf16[32,128,128]{2,1,0:T(8,128)(2,1)S(1)}, u32[]{:S(2)}, u32[]{:S(2)}) %collective-permute-start.20) | collective-permute-done | bytes 1048608 | tf_op jit(solution)/shard_map/ppermute | solution.py:222
  (85 shorter events, 68.7 us)
Async XLA Ops:
  19.9 13.4 %collective-permute-start = (bf16[32,8192]{1,0:T(8,128)(2,1)S(1)}, bf16[32,8192]{1,0:T(8,128)(2,1)}, u32[]{:S(2)}, u32[]{:S(2)}) collective-permute-start(bf16[32,8192]{1,0:T(8,128)(2,1)S(1)} %get-tuple-element.646), channel_id=1, source_target_pairs={{0,8},{8,16},{16,24},{1,9},{9,17},{17,25},{2,10},{10,18},{18,26},{... | collective-permute-start | bytes 1572872 | tf_op jit(solution)/shard_map/ppermute | solution.py:27
  23.1 10.2 %copy-start.1 = (bf16[2,64,8192]{2,1,0:T(8,128)(2,1)S(1)}, bf16[2,64,8192]{2,1,0:T(8,128)(2,1)}, u32[]{:S(2)}) copy-start(bf16[2,64,8192]{2,1,0:T(8,128)(2,1)} %param.44) | copy-start | bytes 6291460
  25.6 25.1 %collective-permute-start.9 = (bf16[32,8192]{1,0:T(8,128)(2,1)S(1)}, bf16[32,8192]{1,0:T(8,128)(2,1)}, u32[]{:S(2)}, u32[]{:S(2)}) collective-permute-start(bf16[32,8192]{1,0:T(8,128)(2,1)S(1)} %get-tuple-element.674), channel_id=1, source_target_pairs={{8,0},{16,8},{24,16},{9,1},{17,9},{25,17},{10,2},{18,10},{26,18},{... | collective-permute-start | bytes 1572872 | tf_op jit(solution)/shard_map/ppermute | solution.py:27
  45.3 15.8 %collective-permute-start.1 = (bf16[32,8192]{1,0:T(8,128)(2,1)S(1)}, bf16[32,8192]{1,0:T(8,128)(2,1)}, u32[]{:S(2)}, u32[]{:S(2)}) collective-permute-start(bf16[32,8192]{1,0:T(8,128)(2,1)S(1)} %get-tuple-element.649), channel_id=1, source_target_pairs={{0,8},{8,16},{16,24},{1,9},{9,17},{17,25},{2,10},{10,18},{18,26},{... | collective-permute-start | bytes 1572872 | tf_op jit(solution)/shard_map/ppermute | solution.py:27
  51.9 29.0 %collective-permute-start.10 = (bf16[32,8192]{1,0:T(8,128)(2,1)S(1)}, bf16[32,8192]{1,0:T(8,128)(2,1)}, u32[]{:S(2)}, u32[]{:S(2)}) collective-permute-start(bf16[32,8192]{1,0:T(8,128)(2,1)S(1)} %get-tuple-element.676), channel_id=1, source_target_pairs={{8,0},{16,8},{24,16},{9,1},{17,9},{25,17},{10,2},{18,10},{26,18},{... | collective-permute-start | bytes 1572872 | tf_op jit(solution)/shard_map/ppermute | solution.py:27
  74.5 15.9 %collective-permute-start.2 = (bf16[32,8192]{1,0:T(8,128)(2,1)S(1)}, bf16[32,8192]{1,0:T(8,128)(2,1)}, u32[]{:S(2)}, u32[]{:S(2)}) collective-permute-start(bf16[32,8192]{1,0:T(8,128)(2,1)S(1)} %get-tuple-element.652), channel_id=1, source_target_pairs={{0,8},{8,16},{16,24},{1,9},{9,17},{17,25},{2,10},{10,18},{18,26},{... | collective-permute-start | bytes 1572872 | tf_op jit(solution)/shard_map/ppermute | solution.py:27
  82.2 25.8 %collective-permute-start.11 = (bf16[32,8192]{1,0:T(8,128)(2,1)S(1)}, bf16[32,8192]{1,0:T(8,128)(2,1)}, u32[]{:S(2)}, u32[]{:S(2)}) collective-permute-start(bf16[32,8192]{1,0:T(8,128)(2,1)S(1)} %get-tuple-element.678), channel_id=1, source_target_pairs={{8,0},{16,8},{24,16},{9,1},{17,9},{25,17},{10,2},{18,10},{26,18},{... | collective-permute-start | bytes 1572872 | tf_op jit(solution)/shard_map/ppermute | solution.py:27
  102.5 14.1 %collective-permute-start.3 = (bf16[32,8192]{1,0:T(8,128)(2,1)S(1)}, bf16[32,8192]{1,0:T(8,128)(2,1)}, u32[]{:S(2)}, u32[]{:S(2)}) collective-permute-start(bf16[32,8192]{1,0:T(8,128)(2,1)S(1)} %get-tuple-element.655), channel_id=1, source_target_pairs={{0,8},{8,16},{16,24},{1,9},{9,17},{17,25},{2,10},{10,18},{18,26},{... | collective-permute-start | bytes 1572872 | tf_op jit(solution)/shard_map/ppermute | solution.py:27
  109.2 25.0 %collective-permute-start.12 = (bf16[32,8192]{1,0:T(8,128)(2,1)S(1)}, bf16[32,8192]{1,0:T(8,128)(2,1)}, u32[]{:S(2)}, u32[]{:S(2)}) collective-permute-start(bf16[32,8192]{1,0:T(8,128)(2,1)S(1)} %get-tuple-element.680), channel_id=1, source_target_pairs={{8,0},{16,8},{24,16},{9,1},{17,9},{25,17},{10,2},{18,10},{26,18},{... | collective-permute-start | bytes 1572872 | tf_op jit(solution)/shard_map/ppermute | solution.py:27
  116.8 25.1 %collective-permute-start.4 = (bf16[32,8192]{1,0:T(8,128)(2,1)S(1)}, bf16[32,8192]{1,0:T(8,128)(2,1)}, u32[]{:S(2)}, u32[]{:S(2)}) collective-permute-start(bf16[32,8192]{1,0:T(8,128)(2,1)S(1)} %get-tuple-element.658), channel_id=1, source_target_pairs={{0,8},{8,16},{16,24},{1,9},{9,17},{17,25},{2,10},{10,18},{18,26},{... | collective-permute-start | bytes 1572872 | tf_op jit(solution)/shard_map/ppermute | solution.py:27
  135.5 14.4 %collective-permute-start.13 = (bf16[32,8192]{1,0:T(8,128)(2,1)S(1)}, bf16[32,8192]{1,0:T(8,128)(2,1)}, u32[]{:S(2)}, u32[]{:S(2)}) collective-permute-start(bf16[32,8192]{1,0:T(8,128)(2,1)S(1)} %get-tuple-element.682), channel_id=1, source_target_pairs={{8,0},{16,8},{24,16},{9,1},{17,9},{25,17},{10,2},{18,10},{26,18},{... | collective-permute-start | bytes 1572872 | tf_op jit(solution)/shard_map/ppermute | solution.py:27
  142.0 15.0 %collective-permute-start.5 = (bf16[32,8192]{1,0:T(8,128)(2,1)S(1)}, bf16[32,8192]{1,0:T(8,128)(2,1)}, u32[]{:S(2)}, u32[]{:S(2)}) collective-permute-start(bf16[32,8192]{1,0:T(8,128)(2,1)S(1)} %get-tuple-element.661), channel_id=1, source_target_pairs={{0,8},{8,16},{16,24},{1,9},{9,17},{17,25},{2,10},{10,18},{18,26},{... | collective-permute-start | bytes 1572872 | tf_op jit(solution)/shard_map/ppermute | solution.py:27
  151.6 52.4 %collective-permute-start.14 = (bf16[32,8192]{1,0:T(8,128)(2,1)S(1)}, bf16[32,8192]{1,0:T(8,128)(2,1)}, u32[]{:S(2)}, u32[]{:S(2)}) collective-permute-start(bf16[32,8192]{1,0:T(8,128)(2,1)S(1)} %get-tuple-element.684), channel_id=1, source_target_pairs={{8,0},{16,8},{24,16},{9,1},{17,9},{25,17},{10,2},{18,10},{26,18},{... | collective-permute-start | bytes 1572872 | tf_op jit(solution)/shard_map/ppermute | solution.py:27
  157.0 65.1 %collective-permute-start.6 = (bf16[32,8192]{1,0:T(8,128)(2,1)S(1)}, bf16[32,8192]{1,0:T(8,128)(2,1)}, u32[]{:S(2)}, u32[]{:S(2)}) collective-permute-start(bf16[32,8192]{1,0:T(8,128)(2,1)S(1)} %get-tuple-element.664), channel_id=1, source_target_pairs={{0,8},{8,16},{16,24},{1,9},{9,17},{17,25},{2,10},{10,18},{18,26},{... | collective-permute-start | bytes 1572872 | tf_op jit(solution)/shard_map/ppermute | solution.py:27
  220.8 13.9 %collective-permute-start.15 = (bf16[32,8192]{1,0:T(8,128)(2,1)S(1)}, bf16[32,8192]{1,0:T(8,128)(2,1)}, u32[]{:S(2)}, u32[]{:S(2)}) collective-permute-start(bf16[32,8192]{1,0:T(8,128)(2,1)S(1)} %get-tuple-element.686), channel_id=1, source_target_pairs={{8,0},{16,8},{24,16},{9,1},{17,9},{25,17},{10,2},{18,10},{26,18},{... | collective-permute-start | bytes 1572872 | tf_op jit(solution)/shard_map/ppermute | solution.py:27
  222.2 32.7 %collective-permute-start.7 = (bf16[32,8192]{1,0:T(8,128)(2,1)S(1)}, bf16[32,8192]{1,0:T(8,128)(2,1)}, u32[]{:S(2)}, u32[]{:S(2)}) collective-permute-start(bf16[32,8192]{1,0:T(8,128)(2,1)S(1)} %get-tuple-element.667), channel_id=1, source_target_pairs={{0,8},{8,16},{16,24},{1,9},{9,17},{17,25},{2,10},{10,18},{18,26},{... | collective-permute-start | bytes 1572872 | tf_op jit(solution)/shard_map/ppermute | solution.py:27
  253.6 19.3 %collective-permute-start.16 = (bf16[32,8192]{1,0:T(8,128)(2,1)}, bf16[32,8192]{1,0:T(8,128)(2,1)S(1)}, u32[]{:S(2)}, u32[]{:S(2)}) collective-permute-start(bf16[32,8192]{1,0:T(8,128)(2,1)} %get-tuple-element.688), channel_id=1, source_target_pairs={{8,0},{16,8},{24,16},{9,1},{17,9},{25,17},{10,2},{18,10},{26,18},{... | collective-permute-start | bytes 1572872 | tf_op jit(solution)/shard_map/ppermute | solution.py:27
  274.0 25.4 %copy-start.3 = (s32[256,3]{0,1:T(4,128)S(1)}, s32[256,3]{0,1:T(4,128)}, u32[]{:S(2)}) copy-start(s32[256,3]{0,1:T(4,128)} %param.47) | copy-start | bytes 9220
  274.0 25.4 %collective-permute-start.8 = (bf16[32,8192]{1,0:T(8,128)(2,1)S(1)}, bf16[32,8192]{1,0:T(8,128)(2,1)}, u32[]{:S(2)}, u32[]{:S(2)}) collective-permute-start(bf16[32,8192]{1,0:T(8,128)(2,1)S(1)} %get-tuple-element.672), channel_id=1, source_target_pairs={{0,8},{8,16},{16,24},{1,9},{9,17},{17,25},{2,10},{10,18},{18,26},{... | collective-permute-start | bytes 1572872 | tf_op jit(solution)/shard_map/ppermute | solution.py:27
  296.5 11.3 %collective-permute-start.17 = (bf16[32,8192]{1,0:T(8,128)(2,1)S(1)}, bf16[32,8192]{1,0:T(8,128)(2,1)}, u32[]{:S(2)}, u32[]{:S(2)}) collective-permute-start(bf16[32,8192]{1,0:T(8,128)(2,1)S(1)} %get-tuple-element.691), channel_id=1, source_target_pairs={{8,0},{16,8},{24,16},{9,1},{17,9},{25,17},{10,2},{18,10},{26,18},{... | collective-permute-start | bytes 1572872 | tf_op jit(solution)/shard_map/ppermute | solution.py:27
  347.9 7.5 %collective-permute-start.18 = (bf16[2,2,32,128,128]{4,3,2,1,0:T(8,128)(2,1)}, bf16[2,2,32,128,128]{4,3,2,1,0:T(8,128)(2,1)}, u32[]{:S(2)}, u32[]{:S(2)}) collective-permute-start(bf16[2,2,32,128,128]{4,3,2,1,0:T(8,128)(2,1)} %fusion), channel_id=1, source_target_pairs={{0,1},{1,0},{2,3},{3,2},{4,5},{5,4},{6,7},{7,6},{8,9},{9,8},{10,11... | collective-permute-start | bytes 12582920 | tf_op jit(solution)/shard_map/ppermute | solution.py:222
  361.3 3.3 copy-start
  365.0 26.2 %collective-permute-start.19 = (bf16[2,32,128,128]{3,2,1,0:T(8,128)(2,1)S(1)}, bf16[2,32,128,128]{3,2,1,0:T(8,128)(2,1)}, u32[]{:S(2)}, u32[]{:S(2)}) collective-permute-start(bf16[2,32,128,128]{3,2,1,0:T(8,128)(2,1)S(1)} %fusion.1), channel_id=1, source_target_pairs={{0,2},{1,5},{2,0},{3,7},{4,6},{5,1},{6,4},{7,3},{8,10},{9,13},{10,... | collective-permute-start | bytes 6291464 | tf_op jit(solution)/shard_map/ppermute | solution.py:222
  396.8 2.0 copy-start.2
  399.0 14.9 %collective-permute-start.20 = (bf16[32,128,128]{2,1,0:T(8,128)(2,1)S(1)}, bf16[32,128,128]{2,1,0:T(8,128)(2,1)S(1)}, u32[]{:S(2)}, u32[]{:S(2)}) collective-permute-start(bf16[32,128,128]{2,1,0:T(8,128)(2,1)S(1)} %fusion.3), channel_id=1, source_target_pairs={{0,4},{1,3},{2,6},{3,1},{4,0},{5,7},{6,2},{7,5},{8,12},{9,11},{10,... | collective-permute-start | bytes 3145736 | tf_op jit(solution)/shard_map/ppermute | solution.py:222

commit v2 on v1

--- a/solution.py
+++ b/solution.py
@@ -12,7 +12,7 @@
 KMAX = 128
 CH = 512
 NSUB = 16
-SPLIT = 2
+SPLIT = 1
 GROUP = 8
 VMEM_LIMIT = 60 * 1024 * 1024
 

time: 421 us -> 456 us (1.083)
  waiting for transfers between devices: 123 us -> 215 us
  Pallas kernels: 115 us -> 76.9 us
  starting transfers between devices: 111 us -> 75.2 us
  loops' own time: 2.15 us -> 17.8 us
  local copies, waits for them, and re-layouts: 35 us -> 27.4 us
  other arithmetic: 30.5 us -> 36.2 us
    ppermute x18 -> x14, waiting for transfers between devices: 74.5 us -> 166 us  [shifted(): lax.ppermute(value, axis, [(source, source + steps) for source in range(l...]
    ppermute x18 -> x14, starting transfers between devices: 111 us -> 75 us  [shifted(): lax.ppermute(value, axis, [(source, source + steps) for source in range(l...]
    pallas_call x8 -> x4, Pallas kernels: 58 us -> 36.2 us  [layer_backward(): pl.pallas_call(functools.partial(_bwd_kernel, layer * KMAX, layer), out_s...]
    pallas_call x8 -> x4, Pallas kernels: 41.7 us -> 24.7 us  [layer_forward(): pl.pallas_call(functools.partial(_fwd_kernel, layer * KMAX, layer), out_s...]
    another operation x10 -> x8, loops' own time: 0.7 us -> 17.5 us  [tick_body(): lax.cond(live_b, run_b, lambda ops: ops, (grad_in, saved_s))]
    select_n x10 -> x8, other arithmetic: 13.8 us -> 18.1 us  [tick_body(): grad_in = jnp.where(me_segment == segments - 1, top, recv_b)]
    another operation x10 -> x6, local copies, waits for them, and re-layouts: 10.8 us -> 7.02 us
  transfers between devices with their start and end apart: 21 -> 17, of which waited for: 13 -> 13; matrix products, arithmetic and copies ran while one was open for 6% -> 5% of each run, Pallas kernels for 18% -> 7%
where the time goes in v2:
time: 456 us; the launch traced here: 449 us
  waiting for transfers between devices  215 us (47%)
  Pallas kernels  76.9 us (17%)
  starting transfers between devices  75.2 us (16%)
  other arithmetic  36.2 us (8%)
  local copies, waits for them, and re-layouts  27.4 us (6%)
  loops' own time  17.8 us (4%)
    ppermute x14, waiting for transfers between devices, shifted(): lax.ppermute(value, axis, [(source, source + steps) for source in range(l...  166 us
    ppermute x14, starting transfers between devices, shifted(): lax.ppermute(value, axis, [(source, source + steps) for source in range(l...  75 us
    ppermute x3, waiting for transfers between devices, _exchange(): lax.ppermute(send.astype(jnp.bfloat16), 'dp', pairs).astype(jnp.float32)  48.4 us
    pallas_call x4, Pallas kernels, layer_backward(): pl.pallas_call(functools.partial(_bwd_kernel, layer * KMAX, layer), out_s...  36.2 us
    pallas_call x4, Pallas kernels, layer_forward(): pl.pallas_call(functools.partial(_fwd_kernel, layer * KMAX, layer), out_s...  24.7 us
    select_n x8, other arithmetic, tick_body(): grad_in = jnp.where(me_segment == segments - 1, top, recv_b)  18.1 us
    another operation x8, loops' own time, tick_body(): lax.cond(live_b, run_b, lambda ops: ops, (grad_in, saved_s))  17.5 us
    pallas_call x1, Pallas kernels, segment_dw(): pl.pallas_call(functools.partial(_dw_kernel, mbs), out_shape=jax.ShapeDty...  16 us
  transfers between devices with their start and end apart: 17, of which 13 were waited for; matrix products, arithmetic and copies ran while one was open for 5% of the time, Pallas kernels for 7%

profile of v2, /device:TPU:0, one launch (start us, length us, event | category | flops | bytes accessed | tf_op | source)
XLA Modules:
  0.0 448.9 jit_solution(2751752097335893825)
XLA Ops:
  1.3 20.9 %conditional.16 = ((bf16[64,8192]{1,0:T(8,128)(2,1)S(1)}, bf16[2,2,64,8192]{3,2,1,0:T(8,128)(2,1)}, f32[2,2,64,8192]{3,2,1,0:T(8,128)})) conditional(s32[]{:T(128)} %convert_element_type.79, bf16[64,8192]{1,0:T(8,128)(2,1)S(1)} %select_bitcast_fusion.1, (s32[]{:T(128)}, s32[256,3]{0,1:T(4,128)}, bf16[64,8192]{1,0:T(8,128)(2,1)S(1)}, ...), branch_computations={%region_0.1_spmd, %region_1.2_spmd} | conditional | bytes 12595214 | solution.py:268
  3.1 4.3 broadcast_in_dim.7.sy_in
  7.4 2.5 broadcast_3_sh_in.0.sh_in
  9.9 6.8 %branch_1_fun.40 = (bf16[64,8192]{1,0:T(8,128)(2,1)}, bf16[2,2,64,8192]{3,2,1,0:T(8,128)(2,1)}, f32[2,2,64,8192]{3,2,1,0:T(8,128)}) custom-call(s32[1]{0:T(128)} %bitcast.at_ref, s32[768]{0:T(1024)} %reshape.83.idx_ref, bf16[64,8192]{1,0:T(8,128)(2,1)S(1)} %get-tuple-element.354.h_ref, ...), custom_call_target="tpu_custom_call", output_to_operand_aliasing={{1}: (4, {}), {2}: (5, {})} | custom-call | tf_op jit(solution)/shard_map/cond/branch_1_fun/pallas_call | solution.py:99
  16.7 5.5 %branch_1_fun.41 = (bf16[64,8192]{1,0:T(8,128)(2,1)S(1)}, bf16[2,2,64,8192]{3,2,1,0:T(8,128)(2,1)}, f32[2,2,64,8192]{3,2,1,0:T(8,128)}) custom-call(s32[1]{0:T(128)} %bitcast.at_ref, s32[768]{0:T(1024)} %reshape.83.idx_ref, bf16[64,8192]{1,0:T(8,128)(2,1)} %get-tuple-element.356.h_ref, ...), custom_call_target="tpu_custom_call", output_to_operand_aliasing={{1}: (4, {}), {2}: (5, {})} | custom-call | tf_op jit(solution)/shard_map/cond/branch_1_fun/pallas_call | solution.py:99
  25.5 2.5 conditional.24
  25.5 2.5 broadcast.18
  29.4 17.4 %collective-permute-done = bf16[64,8192]{1,0:T(8,128)(2,1)} collective-permute-done((bf16[64,8192]{1,0:T(8,128)(2,1)S(1)}, bf16[64,8192]{1,0:T(8,128)(2,1)}, u32[]{:S(2)}, u32[]{:S(2)}) %collective-permute-start) | collective-permute-done | bytes 1048608 | tf_op jit(solution)/shard_map/ppermute | solution.py:27
  46.9 14.2 %conditional.17 = ((bf16[64,8192]{1,0:T(8,128)(2,1)S(1)}, bf16[2,2,64,8192]{3,2,1,0:T(8,128)(2,1)}, f32[2,2,64,8192]{3,2,1,0:T(8,128)})) conditional(s32[]{:T(128)} %convert_element_type.78, (bf16[64,8192]{1,0:T(8,128)(2,1)S(1)}, bf16[2,2,64,8192]{3,2,1,0:T(8,128)(2,1)}, f32[2,2,64,8192]{3,2,1,0:T(8,128)}) %tuple.119, (s32[]{:T(128)}, ...), branch_computations={%region_2.3_spmd, %region_3.4_spmd} | conditional | bytes 12296 | solution.py:268
  48.6 6.8 %branch_1_fun.42 = (bf16[64,8192]{1,0:T(8,128)(2,1)}, bf16[2,2,64,8192]{3,2,1,0:T(8,128)(2,1)}, f32[2,2,64,8192]{3,2,1,0:T(8,128)}) custom-call(s32[1]{0:T(128)} %bitcast.1.at_ref, s32[768]{0:T(1024)} %reshape.89.idx_ref, bf16[64,8192]{1,0:T(8,128)(2,1)S(1)} %get-tuple-element.361.h_ref, ...), custom_call_target="tpu_custom_call", output_to_operand_aliasing={{1}: (4, {}), {2}: (5, {})} | custom-call | tf_op jit(solution)/shard_map/cond/branch_1_fun/pallas_call | solution.py:99
  55.4 5.6 %branch_1_fun.43 = (bf16[64,8192]{1,0:T(8,128)(2,1)S(1)}, bf16[2,2,64,8192]{3,2,1,0:T(8,128)(2,1)}, f32[2,2,64,8192]{3,2,1,0:T(8,128)}) custom-call(s32[1]{0:T(128)} %bitcast.1.at_ref, s32[768]{0:T(1024)} %reshape.89.idx_ref, bf16[64,8192]{1,0:T(8,128)(2,1)} %get-tuple-element.365.h_ref, ...), custom_call_target="tpu_custom_call", output_to_operand_aliasing={{1}: (4, {}), {2}: (5, {})} | custom-call | tf_op jit(solution)/shard_map/cond/branch_1_fun/pallas_call | solution.py:99
  61.2 7.2 %collective-permute-start.1 = (bf16[64,8192]{1,0:T(8,128)(2,1)S(1)}, bf16[64,8192]{1,0:T(8,128)(2,1)}, u32[]{:S(2)}, u32[]{:S(2)}) collective-permute-start(bf16[64,8192]{1,0:T(8,128)(2,1)S(1)} %get-tuple-element.537), channel_id=1, source_target_pairs={{0,8},{8,16},{16,24},{1,9},{9,17},{17,25},{2,10},{10,18},{18,26},{... | collective-permute-start | bytes 3145736 | tf_op jit(solution)/shard_map/ppermute | solution.py:27
  68.4 2.6 bitcast_select_fusion.4
  72.3 17.5 %collective-permute-done.1 = bf16[64,8192]{1,0:T(8,128)(2,1)} collective-permute-done((bf16[64,8192]{1,0:T(8,128)(2,1)S(1)}, bf16[64,8192]{1,0:T(8,128)(2,1)}, u32[]{:S(2)}, u32[]{:S(2)}) %collective-permute-start.1) | collective-permute-done | bytes 1048608 | tf_op jit(solution)/shard_map/ppermute | solution.py:27
  90.0 21.3 %collective-permute-start.2 = (bf16[64,8192]{1,0:T(8,128)(2,1)S(1)}, bf16[64,8192]{1,0:T(8,128)(2,1)}, u32[]{:S(2)}, u32[]{:S(2)}) collective-permute-start(bf16[64,8192]{1,0:T(8,128)(2,1)S(1)} %get-tuple-element.540), channel_id=1, source_target_pairs={{0,8},{8,16},{16,24},{1,9},{9,17},{17,25},{2,10},{10,18},{18,26},{... | collective-permute-start | bytes 3145736 | tf_op jit(solution)/shard_map/ppermute | solution.py:27
  111.3 2.6 bitcast_select_fusion.5
  115.2 16.7 %collective-permute-done.2 = bf16[64,8192]{1,0:T(8,128)(2,1)} collective-permute-done((bf16[64,8192]{1,0:T(8,128)(2,1)S(1)}, bf16[64,8192]{1,0:T(8,128)(2,1)}, u32[]{:S(2)}, u32[]{:S(2)}) %collective-permute-start.2) | collective-permute-done | bytes 1048608 | tf_op jit(solution)/shard_map/ppermute | solution.py:27
  132.0 6.7 %collective-permute-start.3 = (bf16[64,8192]{1,0:T(8,128)(2,1)S(1)}, bf16[64,8192]{1,0:T(8,128)(2,1)}, u32[]{:S(2)}, u32[]{:S(2)}) collective-permute-start(bf16[64,8192]{1,0:T(8,128)(2,1)S(1)} %get-tuple-element.543), channel_id=1, source_target_pairs={{0,8},{8,16},{16,24},{1,9},{9,17},{17,25},{2,10},{10,18},{18,26},{... | collective-permute-start | bytes 3145736 | tf_op jit(solution)/shard_map/ppermute | solution.py:27
  139.9 2.6 bitcast_select_fusion.6
  142.5 8.7 %conditional.27 = ((bf16[64,8192]{1,0:T(8,128)(2,1)}, bf16[2,2,64,8192]{3,2,1,0:T(8,128)(2,1)})) conditional(s32[]{:T(128)} %convert_element_type.84, (bf16[64,8192]{1,0:T(8,128)(2,1)}, bf16[2,2,64,8192]{3,2,1,0:T(8,128)(2,1)}) %tuple.138, (s32[]{:T(128)}, s32[256,3]{0,1:T(4,128)}, bf16[64,8192]{1,0:T(8,128)(2,1)}, f32[2,2,64,8192]{3,2,1,0:T(8,128)}, ...), branch_computations={%region_22.23_spmd, %region_23.24_spmd} | conditional | bytes 12296 | solution.py:284
  152.5 5.8 %collective-permute-done.3 = bf16[64,8192]{1,0:T(8,128)(2,1)} collective-permute-done((bf16[64,8192]{1,0:T(8,128)(2,1)S(1)}, bf16[64,8192]{1,0:T(8,128)(2,1)}, u32[]{:S(2)}, u32[]{:S(2)}) %collective-permute-start.3) | collective-permute-done | bytes 1048608 | tf_op jit(solution)/shard_map/ppermute | solution.py:27
  158.5 17.3 %collective-permute-start.4 = (bf16[64,8192]{1,0:T(8,128)(2,1)S(1)}, bf16[64,8192]{1,0:T(8,128)(2,1)}, u32[]{:S(2)}, u32[]{:S(2)}) collective-permute-start(bf16[64,8192]{1,0:T(8,128)(2,1)S(1)} %get-tuple-element.546), channel_id=1, source_target_pairs={{0,8},{8,16},{16,24},{1,9},{9,17},{17,25},{2,10},{10,18},{18,26},{... | collective-permute-start | bytes 3145736 | tf_op jit(solution)/shard_map/ppermute | solution.py:27
  175.8 9.8 %collective-permute-done.10 = bf16[64,8192]{1,0:T(8,128)(2,1)} collective-permute-done((bf16[64,8192]{1,0:T(8,128)(2,1)}, bf16[64,8192]{1,0:T(8,128)(2,1)}, u32[]{:S(2)}, u32[]{:S(2)}) %collective-permute-start.10) | collective-permute-done | bytes 1048608 | tf_op jit(solution)/shard_map/ppermute | solution.py:27
  185.6 2.6 bitcast_select_fusion.7
  189.5 5.3 %collective-permute-done.4 = bf16[64,8192]{1,0:T(8,128)(2,1)} collective-permute-done((bf16[64,8192]{1,0:T(8,128)(2,1)S(1)}, bf16[64,8192]{1,0:T(8,128)(2,1)}, u32[]{:S(2)}, u32[]{:S(2)}) %collective-permute-start.4) | collective-permute-done | bytes 1048608 | tf_op jit(solution)/shard_map/ppermute | solution.py:27
  194.9 6.7 %collective-permute-start.5 = (bf16[64,8192]{1,0:T(8,128)(2,1)S(1)}, bf16[64,8192]{1,0:T(8,128)(2,1)}, u32[]{:S(2)}, u32[]{:S(2)}) collective-permute-start(bf16[64,8192]{1,0:T(8,128)(2,1)S(1)} %get-tuple-element.549), channel_id=1, source_target_pairs={{0,8},{8,16},{16,24},{1,9},{9,17},{17,25},{2,10},{10,18},{18,26},{... | collective-permute-start | bytes 3145736 | tf_op jit(solution)/shard_map/ppermute | solution.py:27
  201.6 11.3 %collective-permute-done.11 = bf16[64,8192]{1,0:T(8,128)(2,1)} collective-permute-done((bf16[64,8192]{1,0:T(8,128)(2,1)}, bf16[64,8192]{1,0:T(8,128)(2,1)}, u32[]{:S(2)}, u32[]{:S(2)}) %collective-permute-start.11) | collective-permute-done | bytes 1048608 | tf_op jit(solution)/shard_map/ppermute | solution.py:27
  212.9 2.6 bitcast_select_fusion.8
  215.6 8.8 %conditional.29 = ((bf16[64,8192]{1,0:T(8,128)(2,1)}, bf16[2,2,64,8192]{3,2,1,0:T(8,128)(2,1)})) conditional(s32[]{:T(128)} %convert_element_type.82, (bf16[64,8192]{1,0:T(8,128)(2,1)}, bf16[2,2,64,8192]{3,2,1,0:T(8,128)(2,1)}) %tuple.142, (s32[]{:T(128)}, s32[256,3]{0,1:T(4,128)}, bf16[64,8192]{1,0:T(8,128)(2,1)}, f32[2,2,64,8192]{3,2,1,0:T(8,128)}, ...), branch_computations={%region_26.27_spmd, %region_27.28_spmd} | conditional | bytes 12296 | solution.py:284
  226.7 60.2 %collective-permute-done.12 = bf16[64,8192]{1,0:T(8,128)(2,1)S(1)} collective-permute-done((bf16[64,8192]{1,0:T(8,128)(2,1)}, bf16[64,8192]{1,0:T(8,128)(2,1)S(1)}, u32[]{:S(2)}, u32[]{:S(2)}) %collective-permute-start.12) | collective-permute-done | bytes 1048608 | tf_op jit(solution)/shard_map/ppermute | solution.py:27
  288.3 4.6 %collective-permute-start.6 = (bf16[64,8192]{1,0:T(8,128)(2,1)}, bf16[64,8192]{1,0:T(8,128)(2,1)}, u32[]{:S(2)}, u32[]{:S(2)}) collective-permute-start(bf16[64,8192]{1,0:T(8,128)(2,1)} %get-tuple-element.554), channel_id=1, source_target_pairs={{0,8},{8,16},{16,24},{1,9},{9,17},{17,25},{2,10},{10,18},{18,26},{... | collective-permute-start | bytes 3145736 | tf_op jit(solution)/shard_map/ppermute | solution.py:27
  293.0 18.3 %conditional.30 = ((bf16[64,8192]{1,0:T(8,128)(2,1)S(1)}, bf16[2,2,64,8192]{3,2,1,0:T(8,128)(2,1)})) conditional(s32[]{:T(128)} %convert_element_type.81, (bf16[64,8192]{1,0:T(8,128)(2,1)S(1)}, bf16[2,2,64,8192]{3,2,1,0:T(8,128)(2,1)}) %tuple.144, (s32[]{:T(128)}, s32[256,3]{0,1:T(4,128)S(1)}, bf16[64,8192]{1,0:T(8,128)(2,1)S(1)}, ...), branch_computations={%region_28.29_spmd.clone, %region_29.30_spmd.clone} | conditional | bytes 12296 | solution.py:284
  293.9 8.2 %branch_1_fun.70 = (bf16[64,8192]{1,0:T(8,128)(2,1)}, bf16[2,2,64,8192]{3,2,1,0:T(8,128)(2,1)}) custom-call(s32[1]{0:T(128)} %bitcast.40.at_ref, s32[768]{0:T(1024)} %reshape.145.idx_ref, bf16[64,8192]{1,0:T(8,128)(2,1)S(1)} %get-tuple-element.578.g_ref, f32[2,2,64,8192]{3,2,1,0:T(8,128)} %get-tuple-element.579.sy_hbm, ...), custom_call_target="tpu_custom_call", output_to_operand_aliasing={{1}: (5, {})} | custom-call | tf_op jit(solution)/shard_map/cond/branch_1_fun/pallas_call | solution.py:166
  302.1 9.2 %branch_1_fun.71 = (bf16[64,8192]{1,0:T(8,128)(2,1)S(1)}, bf16[2,2,64,8192]{3,2,1,0:T(8,128)(2,1)}) custom-call(s32[1]{0:T(128)} %bitcast.40.at_ref, s32[768]{0:T(1024)} %reshape.145.idx_ref, bf16[64,8192]{1,0:T(8,128)(2,1)} %get-tuple-element.582.g_ref, f32[2,2,64,8192]{3,2,1,0:T(8,128)} %get-tuple-element.579.sy_hbm, ...), custom_call_target="tpu_custom_call", output_to_operand_aliasing={{1}: (5, {})} | custom-call | tf_op jit(solution)/shard_map/cond/branch_1_fun/pallas_call | solution.py:166
  313.5 21.0 %collective-permute-done.13 = bf16[64,8192]{1,0:T(8,128)(2,1)} collective-permute-done((bf16[64,8192]{1,0:T(8,128)(2,1)S(1)}, bf16[64,8192]{1,0:T(8,128)(2,1)}, u32[]{:S(2)}, u32[]{:S(2)}) %collective-permute-start.13) | collective-permute-done | bytes 1048608 | tf_op jit(solution)/shard_map/ppermute | solution.py:27
  334.6 22.4 %conditional.31 = (bf16[2,2,64,8192]{3,2,1,0:T(8,128)(2,1)}) conditional(s32[]{:T(128)} %convert_element_type.80, bf16[2,2,64,8192]{3,2,1,0:T(8,128)(2,1)} %get-tuple-element.568, (s32[]{:T(128)}, s32[256,3]{0,1:T(4,128)S(1)}, pred[]{:T(512)}, bf16[2,64,8192]{2,1,0:T(8,128)(2,1)}, bf16[64,8192]{1,0:T(8,128)(2,1)}, ...), branch_computations={%region_30.31_spmd, %region_31.32_spmd} | conditional | flops 524290 | bytes 3158053 | solution.py:284
  334.6 2.6 bitcast_select_fusion.1.g_ref
  338.1 8.7 %branch_1_fun.68 = (bf16[64,8192]{1,0:T(8,128)(2,1)}, bf16[2,2,64,8192]{3,2,1,0:T(8,128)(2,1)}) custom-call(s32[1]{0:T(128)} %bitcast.15.at_ref, s32[768]{0:T(1024)} %reshape.139.idx_ref, bf16[64,8192]{1,0:T(8,128)(2,1)} %bitcast_select_fusion.1.g_ref, f32[2,2,64,8192]{3,2,1,0:T(8,128)} %get-tuple-element.490.sy_hbm, ...), custom_call_target="tpu_custom_call", output_to_operand_aliasing={{1}: (5, {})} | custom-call | tf_op jit(solution)/shard_map/cond/branch_1_fun/pallas_call | solution.py:166
  346.9 10.1 %branch_1_fun.69 = (bf16[64,8192]{1,0:T(8,128)(2,1)}, bf16[2,2,64,8192]{3,2,1,0:T(8,128)(2,1)}) custom-call(s32[1]{0:T(128)} %bitcast.15.at_ref, s32[768]{0:T(1024)} %reshape.139.idx_ref, bf16[64,8192]{1,0:T(8,128)(2,1)} %get-tuple-element.493.g_ref, f32[2,2,64,8192]{3,2,1,0:T(8,128)} %get-tuple-element.490.sy_hbm, ...), custom_call_target="tpu_custom_call", output_to_operand_aliasing={{1}: (5, {})} | custom-call | tf_op jit(solution)/shard_map/cond/branch_1_fun/pallas_call | solution.py:166
  357.0 16.0 %shard_map.46 = f32[256,128,128]{2,1,0:T(8,128)} custom-call(s32[768]{0:T(1024)} %reshape.142.idx_ref, bf16[2,2,64,8192]{3,2,1,0:T(8,128)(2,1)} %get-tuple-element.555.h_ref, bf16[2,2,64,8192]{3,2,1,0:T(8,128)(2,1)} %get-tuple-element.774.s_ref), custom_call_target="tpu_custom_call" | custom-call | tf_op jit(solution)/shard_map/pallas_call | solution.py:212
  373.0 6.4 %fusion = bf16[2,2,32,128,128]{4,3,2,1,0:T(8,128)(2,1)} fusion(f32[2,2,2,32,128,128]{5,4,3,2,1,0:T(8,128)} %bitcast.69, s32[]{:T(128)S(6)} %select_n.199), kind=kLoop, calls=%fused_computation.4 | loop fusion | bytes 8388612 | tf_op jit(solution)/shard_map/convert_element_type | solution.py:222
  379.4 7.5 %collective-permute-done.14 = bf16[2,2,32,128,128]{4,3,2,1,0:T(8,128)(2,1)} collective-permute-done((bf16[2,2,32,128,128]{4,3,2,1,0:T(8,128)(2,1)}, bf16[2,2,32,128,128]{4,3,2,1,0:T(8,128)(2,1)}, u32[]{:S(2)}, u32[]{:S(2)}) %collective-permute-start.14) | collective-permute-done | bytes 4194336 | tf_op jit(solution)/shard_map/ppermute | solution.py:222
  386.9 5.9 %bitcast_add_fusion = f32[2,2,32,128,128]{4,3,2,1,0:T(8,128)S(1)} fusion(bf16[2,2,32,128,128]{4,3,2,1,0:T(8,128)(2,1)} %collective-permute-done.14, f32[2,2,2,32,128,128]{5,4,3,2,1,0:T(8,128)} %bitcast.70, s32[]{:T(128)S(6)} %select_n.198), kind=kLoop, calls=%fused_computation.2 | loop fusion | flops 4194304 | bytes 20971524 | tf_op jit(solution)/shard_map/add | solution.py:235
  392.9 3.4 copy-done
  396.7 26.1 %collective-permute-done.15 = bf16[2,32,128,128]{3,2,1,0:T(8,128)(2,1)} collective-permute-done((bf16[2,32,128,128]{3,2,1,0:T(8,128)(2,1)S(1)}, bf16[2,32,128,128]{3,2,1,0:T(8,128)(2,1)}, u32[]{:S(2)}, u32[]{:S(2)}) %collective-permute-start.15) | collective-permute-done | bytes 2097184 | tf_op jit(solution)/shard_map/ppermute | solution.py:222
  422.8 5.6 %fusion.2 = f32[2,32,128,128]{3,2,1,0:T(8,128)S(1)} fusion(bf16[2,32,128,128]{3,2,1,0:T(8,128)(2,1)} %collective-permute-done.15, f32[2,2,32,128,128]{4,3,2,1,0:T(8,128)} %copy-done, s32[]{:T(128)S(6)} %select_n.204, s32[]{:T(128)S(6)} %select_n.202, pred[]{:T(512)S(6)} %eq.8), kind=kLoop, calls=%fused_computation.8 | loop fusion | flops 3145728 | bytes 14680073 | tf_op jit(solution)/shard_map/add | solution.py:239
  430.6 14.8 %collective-permute-done.16 = bf16[32,128,128]{2,1,0:T(8,128)(2,1)S(1)} collective-permute-done((bf16[32,128,128]{2,1,0:T(8,128)(2,1)S(1)}, bf16[32,128,128]{2,1,0:T(8,128)(2,1)S(1)}, u32[]{:S(2)}, u32[]{:S(2)}) %collective-permute-start.16) | collective-permute-done | bytes 1048608 | tf_op jit(solution)/shard_map/ppermute | solution.py:222
  445.4 3.3 bitcast_add_fusion.1
  (55 shorter events, 26.7 us)
Async XLA Ops:
  1.3 23.2 %copy-start.2 = (bf16[2,64,8192]{2,1,0:T(8,128)(2,1)S(1)}, bf16[2,64,8192]{2,1,0:T(8,128)(2,1)}, u32[]{:S(2)}) copy-start(bf16[2,64,8192]{2,1,0:T(8,128)(2,1)} %param.37) | copy-start | bytes 6291460
  22.2 24.6 %collective-permute-start = (bf16[64,8192]{1,0:T(8,128)(2,1)S(1)}, bf16[64,8192]{1,0:T(8,128)(2,1)}, u32[]{:S(2)}, u32[]{:S(2)}) collective-permute-start(bf16[64,8192]{1,0:T(8,128)(2,1)S(1)} %get-tuple-element.534), channel_id=1, source_target_pairs={{0,8},{8,16},{16,24},{1,9},{9,17},{17,25},{2,10},{10,18},{18,26},{... | collective-permute-start | bytes 3145736 | tf_op jit(solution)/shard_map/ppermute | solution.py:27
  25.5 21.3 %copy-start.1 = (bf16[2,64,8192]{2,1,0:T(8,128)(2,1)S(1)}, bf16[2,64,8192]{2,1,0:T(8,128)(2,1)}, u32[]{:S(2)}) copy-start(bf16[2,64,8192]{2,1,0:T(8,128)(2,1)} %param.36) | copy-start | bytes 6291460
  28.0 40.3 %collective-permute-start.7 = (bf16[64,8192]{1,0:T(8,128)(2,1)}, bf16[64,8192]{1,0:T(8,128)(2,1)}, u32[]{:S(2)}, u32[]{:S(2)}) collective-permute-start(bf16[64,8192]{1,0:T(8,128)(2,1)} %get-tuple-element.556), channel_id=1, source_target_pairs={{8,0},{16,8},{24,16},{9,1},{17,9},{25,17},{10,2},{18,10},{26,18},{... | collective-permute-start | bytes 3145736 | tf_op jit(solution)/shard_map/ppermute | solution.py:27
  61.2 28.6 %collective-permute-start.1 = (bf16[64,8192]{1,0:T(8,128)(2,1)S(1)}, bf16[64,8192]{1,0:T(8,128)(2,1)}, u32[]{:S(2)}, u32[]{:S(2)}) collective-permute-start(bf16[64,8192]{1,0:T(8,128)(2,1)S(1)} %get-tuple-element.537), channel_id=1, source_target_pairs={{0,8},{8,16},{16,24},{1,9},{9,17},{17,25},{2,10},{10,18},{18,26},{... | collective-permute-start | bytes 3145736 | tf_op jit(solution)/shard_map/ppermute | solution.py:27
  71.0 40.3 %collective-permute-start.8 = (bf16[64,8192]{1,0:T(8,128)(2,1)}, bf16[64,8192]{1,0:T(8,128)(2,1)}, u32[]{:S(2)}, u32[]{:S(2)}) collective-permute-start(bf16[64,8192]{1,0:T(8,128)(2,1)} %get-tuple-element.558), channel_id=1, source_target_pairs={{8,0},{16,8},{24,16},{9,1},{17,9},{25,17},{10,2},{18,10},{26,18},{... | collective-permute-start | bytes 3145736 | tf_op jit(solution)/shard_map/ppermute | solution.py:27
  90.0 41.9 %collective-permute-start.2 = (bf16[64,8192]{1,0:T(8,128)(2,1)S(1)}, bf16[64,8192]{1,0:T(8,128)(2,1)}, u32[]{:S(2)}, u32[]{:S(2)}) collective-permute-start(bf16[64,8192]{1,0:T(8,128)(2,1)S(1)} %get-tuple-element.540), channel_id=1, source_target_pairs={{0,8},{8,16},{16,24},{1,9},{9,17},{17,25},{2,10},{10,18},{18,26},{... | collective-permute-start | bytes 3145736 | tf_op jit(solution)/shard_map/ppermute | solution.py:27
  113.9 26.0 %collective-permute-start.9 = (bf16[64,8192]{1,0:T(8,128)(2,1)}, bf16[64,8192]{1,0:T(8,128)(2,1)}, u32[]{:S(2)}, u32[]{:S(2)}) collective-permute-start(bf16[64,8192]{1,0:T(8,128)(2,1)} %get-tuple-element.560), channel_id=1, source_target_pairs={{8,0},{16,8},{24,16},{9,1},{17,9},{25,17},{10,2},{18,10},{26,18},{... | collective-permute-start | bytes 3145736 | tf_op jit(solution)/shard_map/ppermute | solution.py:27
  132.0 26.4 %collective-permute-start.3 = (bf16[64,8192]{1,0:T(8,128)(2,1)S(1)}, bf16[64,8192]{1,0:T(8,128)(2,1)}, u32[]{:S(2)}, u32[]{:S(2)}) collective-permute-start(bf16[64,8192]{1,0:T(8,128)(2,1)S(1)} %get-tuple-element.543), channel_id=1, source_target_pairs={{0,8},{8,16},{16,24},{1,9},{9,17},{17,25},{2,10},{10,18},{18,26},{... | collective-permute-start | bytes 3145736 | tf_op jit(solution)/shard_map/ppermute | solution.py:27
  151.2 34.4 %collective-permute-start.10 = (bf16[64,8192]{1,0:T(8,128)(2,1)}, bf16[64,8192]{1,0:T(8,128)(2,1)}, u32[]{:S(2)}, u32[]{:S(2)}) collective-permute-start(bf16[64,8192]{1,0:T(8,128)(2,1)} %get-tuple-element.562), channel_id=1, source_target_pairs={{8,0},{16,8},{24,16},{9,1},{17,9},{25,17},{10,2},{18,10},{26,18},{... | collective-permute-start | bytes 3145736 | tf_op jit(solution)/shard_map/ppermute | solution.py:27
  158.5 36.3 %collective-permute-start.4 = (bf16[64,8192]{1,0:T(8,128)(2,1)S(1)}, bf16[64,8192]{1,0:T(8,128)(2,1)}, u32[]{:S(2)}, u32[]{:S(2)}) collective-permute-start(bf16[64,8192]{1,0:T(8,128)(2,1)S(1)} %get-tuple-element.546), channel_id=1, source_target_pairs={{0,8},{8,16},{16,24},{1,9},{9,17},{17,25},{2,10},{10,18},{18,26},{... | collective-permute-start | bytes 3145736 | tf_op jit(solution)/shard_map/ppermute | solution.py:27
  188.2 24.7 %collective-permute-start.11 = (bf16[64,8192]{1,0:T(8,128)(2,1)}, bf16[64,8192]{1,0:T(8,128)(2,1)}, u32[]{:S(2)}, u32[]{:S(2)}) collective-permute-start(bf16[64,8192]{1,0:T(8,128)(2,1)} %get-tuple-element.564), channel_id=1, source_target_pairs={{8,0},{16,8},{24,16},{9,1},{17,9},{25,17},{10,2},{18,10},{26,18},{... | collective-permute-start | bytes 3145736 | tf_op jit(solution)/shard_map/ppermute | solution.py:27
  194.9 30.7 %collective-permute-start.5 = (bf16[64,8192]{1,0:T(8,128)(2,1)S(1)}, bf16[64,8192]{1,0:T(8,128)(2,1)}, u32[]{:S(2)}, u32[]{:S(2)}) collective-permute-start(bf16[64,8192]{1,0:T(8,128)(2,1)S(1)} %get-tuple-element.549), channel_id=1, source_target_pairs={{0,8},{8,16},{16,24},{1,9},{9,17},{17,25},{2,10},{10,18},{18,26},{... | collective-permute-start | bytes 3145736 | tf_op jit(solution)/shard_map/ppermute | solution.py:27
  224.3 64.0 %copy-start.4 = (s32[256,3]{0,1:T(4,128)S(1)}, s32[256,3]{0,1:T(4,128)}, u32[]{:S(2)}) copy-start(s32[256,3]{0,1:T(4,128)} %param.39) | copy-start | bytes 9220
  224.3 62.6 %collective-permute-start.12 = (bf16[64,8192]{1,0:T(8,128)(2,1)}, bf16[64,8192]{1,0:T(8,128)(2,1)S(1)}, u32[]{:S(2)}, u32[]{:S(2)}) collective-permute-start(bf16[64,8192]{1,0:T(8,128)(2,1)} %get-tuple-element.566), channel_id=1, source_target_pairs={{8,0},{16,8},{24,16},{9,1},{17,9},{25,17},{10,2},{18,10},{26,18},{... | collective-permute-start | bytes 3145736 | tf_op jit(solution)/shard_map/ppermute | solution.py:27
  288.3 25.2 %collective-permute-start.6 = (bf16[64,8192]{1,0:T(8,128)(2,1)}, bf16[64,8192]{1,0:T(8,128)(2,1)}, u32[]{:S(2)}, u32[]{:S(2)}) collective-permute-start(bf16[64,8192]{1,0:T(8,128)(2,1)} %get-tuple-element.554), channel_id=1, source_target_pairs={{0,8},{8,16},{16,24},{1,9},{9,17},{17,25},{2,10},{10,18},{18,26},{... | collective-permute-start | bytes 3145736 | tf_op jit(solution)/shard_map/ppermute | solution.py:27
  311.3 23.3 %collective-permute-start.13 = (bf16[64,8192]{1,0:T(8,128)(2,1)S(1)}, bf16[64,8192]{1,0:T(8,128)(2,1)}, u32[]{:S(2)}, u32[]{:S(2)}) collective-permute-start(bf16[64,8192]{1,0:T(8,128)(2,1)S(1)} %get-tuple-element.569), channel_id=1, source_target_pairs={{8,0},{16,8},{24,16},{9,1},{17,9},{25,17},{10,2},{18,10},{26,18},{... | collective-permute-start | bytes 3145736 | tf_op jit(solution)/shard_map/ppermute | solution.py:27
  379.4 7.5 %collective-permute-start.14 = (bf16[2,2,32,128,128]{4,3,2,1,0:T(8,128)(2,1)}, bf16[2,2,32,128,128]{4,3,2,1,0:T(8,128)(2,1)}, u32[]{:S(2)}, u32[]{:S(2)}) collective-permute-start(bf16[2,2,32,128,128]{4,3,2,1,0:T(8,128)(2,1)} %fusion), channel_id=1, source_target_pairs={{0,1},{1,0},{2,3},{3,2},{4,5},{5,4},{6,7},{7,6},{8,9},{9,8},{10,11... | collective-permute-start | bytes 12582920 | tf_op jit(solution)/shard_map/ppermute | solution.py:222
  392.8 3.4 copy-start
  396.6 26.2 %collective-permute-start.15 = (bf16[2,32,128,128]{3,2,1,0:T(8,128)(2,1)S(1)}, bf16[2,32,128,128]{3,2,1,0:T(8,128)(2,1)}, u32[]{:S(2)}, u32[]{:S(2)}) collective-permute-start(bf16[2,32,128,128]{3,2,1,0:T(8,128)(2,1)S(1)} %fusion.1), channel_id=1, source_target_pairs={{0,2},{1,5},{2,0},{3,7},{4,6},{5,1},{6,4},{7,3},{8,10},{9,13},{10,... | collective-permute-start | bytes 6291464 | tf_op jit(solution)/shard_map/ppermute | solution.py:222
  428.4 2.0 copy-start.3
  430.5 14.9 %collective-permute-start.16 = (bf16[32,128,128]{2,1,0:T(8,128)(2,1)S(1)}, bf16[32,128,128]{2,1,0:T(8,128)(2,1)S(1)}, u32[]{:S(2)}, u32[]{:S(2)}) collective-permute-start(bf16[32,128,128]{2,1,0:T(8,128)(2,1)S(1)} %fusion.3), channel_id=1, source_target_pairs={{0,4},{1,3},{2,6},{3,1},{4,0},{5,7},{6,2},{7,5},{8,12},{9,11},{10,... | collective-permute-start | bytes 3145736 | tf_op jit(solution)/shard_map/ppermute | solution.py:222
